TPU v7x, 32 devices: a whole 2x2x4 slice. The times are simulated.
32 devices in a mesh: tok: 8 (over z, core), head: 4 (over y, x).
Axes of the slice: x: 2, y: 2, z: 4, core: 2. Of those that a mesh axis runs over, the one named last changes fastest.
Arguments:
- query_states: bfloat16 [12288, 3072], P('tok', 'head')
- key_states: bfloat16 [12288, 3072], P('tok', 'head')
- value_states: bfloat16 [12288, 3072], P('tok', 'head'), may hold values from -6 to 6
- query_gain: float32 [3072], P('head'), may hold values from 1 to 2.5
- key_gain: float32 [3072], P('head'), may hold values from 1 to 2.5
- windows: int32 [48, 27], P('tok'), may hold values from -1 to 47, as said below
Outputs:
- attention: bfloat16 [12288, 3072], P('tok', 'head')
Inputs may be any that keep to these rules, and one draw needn't show every extreme that they name: Slots 0 to 8 of windows[i] name tiles of the tile-frame before tile i's, the next 9 tiles of its own tile-frame, the last 9 tiles of the tile-frame after it; in each group the named tiles come first and -1 fills the rest; tile i itself is always named; no tile is named twice in a row; a named tile's tile row and tile column differ from tile i's by at most 2 each, and some named tiles differ by 2 in both.
All inputs are finite; a program needn't handle non-finite values.
Results may differ from a plain program's by a relative error of at most 0.012.
The roundings to bfloat16 on the way count: a program that leaves them out, or rounds other values in their place, can miss the bound.
Values may be sent and summed in bfloat16 or wider, within the bound.
No kernel may reach another device: no remote copies, remote signals or barrier semaphores. Data moves between devices by JAX's collectives and lax.ppermute only.
A program may use at most 320 MiB of HBM per device.

v0:
```python
import functools
import math

import jax
import jax.numpy as jnp
from jax import lax
from jax.experimental import pallas as pl
from jax.experimental.pallas import tpu as pltpu
from jax.sharding import PartitionSpec as P

HEAD_DIM = 128
MODEL_DIM = 3072
TILE_TOKENS = 256
WINDOW_SLOTS = 27
SLOTS_PER_STEP = 1
STATS_HALF = 64


def square_sums(source):
    widened = source.astype(jnp.float32)
    return jnp.sum(widened * widened, axis=1)


def normalize_rows(source, totals, scale_gain):
    widened = source.astype(jnp.float32)
    return (widened * lax.rsqrt(totals[:, None] / MODEL_DIM + 1e-06) * scale_gain).astype(
        jnp.bfloat16
    )


def compact_windows(windows, tile_count):
    valid = windows >= 0
    order = jnp.argsort(jnp.logical_not(valid).astype(jnp.int32), axis=1, stable=True)
    ids = jnp.take_along_axis(windows, order, axis=1)
    counts = jnp.sum(valid.astype(jnp.int32), axis=1)
    last = jnp.take_along_axis(ids, jnp.maximum(counts - 1, 0)[:, None], axis=1)
    slot = lax.broadcasted_iota(jnp.int32, ids.shape, 1)
    ids = jnp.where(slot < counts[:, None], ids, last)
    ids = jnp.clip(ids, 0, tile_count - 1)
    return ids.reshape(-1).astype(jnp.int32), counts.astype(jnp.int32)


def attention_kernel(ids_ref, cnt_ref, q_ref, *refs, first, last):
    k_refs = refs[:SLOTS_PER_STEP]
    v_refs = refs[SLOTS_PER_STEP:2 * SLOTS_PER_STEP]
    rest = refs[2 * SLOTS_PER_STEP:]
    if not first:
        acc_in, stats_in = rest[:2]
        rest = rest[2:]
    if last:
        o_ref = rest[0]
        rest = rest[1:]
    else:
        acc_out, stats_out = rest[:2]
        rest = rest[2:]
    m_sc, l_sc, acc_sc = rest
    t = pl.program_id(0)
    j = pl.program_id(1)
    heads = q_ref.shape[0] // HEAD_DIM
    score_scale = 1.0 / math.sqrt(HEAD_DIM)

    @pl.when(j == 0)
    def _init():
        if first:
            m_sc[...] = jnp.full(m_sc.shape, -jnp.inf, jnp.float32)
            l_sc[...] = jnp.zeros(l_sc.shape, jnp.float32)
            acc_sc[...] = jnp.zeros(acc_sc.shape, jnp.float32)
        else:
            m_sc[...] = stats_in[0, 0]
            l_sc[...] = stats_in[0, 1]
            acc_sc[...] = acc_in[0]

    for sub in range(SLOTS_PER_STEP):
        k_ref = k_refs[sub]
        v_ref = v_refs[sub]

        @pl.when(j * SLOTS_PER_STEP + sub < cnt_ref[t])
        def _step():
            for h in range(heads):
                cols = slice(h * HEAD_DIM, (h + 1) * HEAD_DIM)
                q_t = q_ref[cols, :]
                k = k_ref[0, :, cols]
                v = v_ref[0, :, cols]
                scores = (
                    lax.dot_general(
                        k, q_t, (((1,), (0,)), ((), ())), preferred_element_type=jnp.float32
                    )
                    * score_scale
                )
                m_prev = m_sc[h]
                m_cur = jnp.max(scores, axis=0, keepdims=True)
                m_new = jnp.maximum(m_prev, m_cur)
                alpha = jnp.exp(m_prev - m_new)
                weights = jnp.exp(scores - m_new)
                l_sc[h] = alpha * l_sc[h] + jnp.sum(weights, axis=0, keepdims=True)
                m_sc[h] = m_new
                mixed = lax.dot_general(
                    v, weights.astype(jnp.bfloat16), (((0,), (0,)), ((), ())),
                    preferred_element_type=jnp.float32,
                )
                acc_sc[cols, :] = acc_sc[cols, :] * alpha + mixed

    @pl.when(j == pl.num_programs(1) - 1)
    def _finish():
        if last:
            for h in range(heads):
                cols = slice(h * HEAD_DIM, (h + 1) * HEAD_DIM)
                o_ref[:, cols] = (acc_sc[cols, :] / l_sc[h]).T.astype(o_ref.dtype)
        else:
            acc_out[0] = acc_sc[...]
            stats_out[0, 0] = m_sc[...]
            stats_out[0, 1] = l_sc[...]


def window_attention(query_t, paired, ids, counts, state, last):
    width, rows = query_t.shape
    local_tiles = rows // TILE_TOKENS
    heads = width // HEAD_DIM
    steps = WINDOW_SLOTS // SLOTS_PER_STEP
    first = state is None

    def window_spec(lead, sub):
        return pl.BlockSpec(
            (1, TILE_TOKENS, width),
            lambda t, j, ids, cnt: (lead, ids[t * WINDOW_SLOTS + j * SLOTS_PER_STEP + sub], 0),
        )

    acc_spec = pl.BlockSpec((1, width, TILE_TOKENS), lambda t, j, ids, cnt: (t, 0, 0))
    stats_spec = pl.BlockSpec(
        (1, 2, heads, 1, TILE_TOKENS), lambda t, j, ids, cnt: (t, 0, 0, 0, 0)
    )
    in_specs = [pl.BlockSpec((width, TILE_TOKENS), lambda t, j, ids, cnt: (0, t))]
    in_specs += [window_spec(0, sub) for sub in range(SLOTS_PER_STEP)]
    in_specs += [window_spec(1, sub) for sub in range(SLOTS_PER_STEP)]
    operands = [ids, counts, query_t] + [paired] * (2 * SLOTS_PER_STEP)
    if not first:
        in_specs += [acc_spec, stats_spec]
        operands += list(state)
    if last:
        out_specs = pl.BlockSpec((TILE_TOKENS, width), lambda t, j, ids, cnt: (t, 0))
        out_shape = jax.ShapeDtypeStruct((rows, width), jnp.bfloat16)
    else:
        out_specs = [acc_spec, stats_spec]
        out_shape = [
            jax.ShapeDtypeStruct((local_tiles, width, TILE_TOKENS), jnp.float32),
            jax.ShapeDtypeStruct((local_tiles, 2, heads, 1, TILE_TOKENS), jnp.float32),
        ]
    grid_spec = pltpu.PrefetchScalarGridSpec(
        num_scalar_prefetch=2,
        grid=(local_tiles, steps),
        in_specs=in_specs,
        out_specs=out_specs,
        scratch_shapes=[
            pltpu.VMEM((heads, 1, TILE_TOKENS), jnp.float32),
            pltpu.VMEM((heads, 1, TILE_TOKENS), jnp.float32),
            pltpu.VMEM((width, TILE_TOKENS), jnp.float32),
        ],
    )
    return pl.pallas_call(
        functools.partial(attention_kernel, first=first, last=last),
        grid_spec=grid_spec,
        out_shape=out_shape,
        compiler_params=pltpu.CompilerParams(
            dimension_semantics=("arbitrary", "arbitrary")
        ),
    )(*operands)


def phase_windows(windows, local_tiles, start, size, tile_count):
    safe = jnp.clip(windows, 0, tile_count - 1)
    position = safe % local_tiles
    inside = (windows >= 0) & (position >= start) & (position < start + size)
    block = (safe // local_tiles) * size + jnp.clip(position - start, 0, size - 1)
    order = jnp.argsort(jnp.logical_not(inside).astype(jnp.int32), axis=1, stable=True)
    ids = jnp.take_along_axis(block, order, axis=1)
    counts = jnp.sum(inside.astype(jnp.int32), axis=1)
    last = jnp.take_along_axis(ids, jnp.maximum(counts - 1, 0)[:, None], axis=1)
    slot = lax.broadcasted_iota(jnp.int32, ids.shape, 1)
    ids = jnp.where(slot < counts[:, None], ids, last)
    ids = jnp.clip(ids, 0, (tile_count // local_tiles) * size - 1)
    return ids.reshape(-1).astype(jnp.int32), counts.astype(jnp.int32)


def phase_sizes(local_tiles):
    if local_tiles >= 3:
        return [1, 2] + [1] * (local_tiles - 3)
    return [local_tiles]


def on_device(query_states, key_states, value_states, query_gain, key_gain, windows, tok_count):
    rows = query_states.shape[0]
    local_tiles = rows // TILE_TOKENS
    tile_count = tok_count * local_tiles
    sizes = phase_sizes(local_tiles)
    query_total, key_total = lax.psum((square_sums(query_states), square_sums(key_states)), "head")
    query_normed = normalize_rows(query_states, query_total, query_gain)
    sent_keys = normalize_rows(key_states, key_total, key_gain)
    query_t = query_normed.T
    state = None
    start = 0
    for number, size in enumerate(sizes):
        part = slice(start * TILE_TOKENS, (start + size) * TILE_TOKENS)
        paired = jnp.stack([sent_keys[part], value_states[part]])
        extended = lax.all_gather(paired, "tok", axis=1, tiled=True)
        ids, counts = phase_windows(windows, local_tiles, start, size, tile_count)
        state = window_attention(
            query_t, extended, ids, counts, state, number == len(sizes) - 1
        )
        start += size
    return state


def solution(mesh):
    in_specs = (
        P("tok", "head"),
        P("tok", "head"),
        P("tok", "head"),
        P("head"),
        P("head"),
        P("tok", None),
    )
    out_specs = P("tok", "head")
    return jax.shard_map(
        functools.partial(on_device, tok_count=mesh.shape["tok"]),
        mesh=mesh,
        in_specs=in_specs,
        out_specs=out_specs,
        check_vma=False,
    )
```

profile of v0, /device:TPU:11, one launch (start us, length us, event | category | flops | bytes accessed | tf_op | source)
XLA Modules:
  0.0 486.5 jit_solution(10577764636113158047)
XLA Ops:
  6.5 2.8 copy.12
  9.4 0.5 fusion
  9.9 2.2 fusion.3
  12.1 10.6 %all-reduce = (f32[1536]{0:T(1024)S(1)}, f32[1536]{0:T(1024)S(1)}) all-reduce(f32[1536]{0:T(1024)S(1)} %fusion, f32[1536]{0:T(1024)S(1)} %fusion.3), channel_id=1, replica_groups=mesh['tok'=8,'head'=4] {'head'}, use_global_device_ids=true, to_apply=%region_3.6 | all-reduce | flops 3072 | bytes 24576 | tf_op jit(solution)/shard_map/psum | solution.py:195
  22.7 2.4 fusion.5
  25.1 1.4 copy-done
  26.5 1.1 slice_bitcast_fusion.2
  27.6 1.0 pad_maximum_fusion.4
  28.7 1.2 slice_bitcast_fusion
  29.8 1.2 slice_bitcast_fusion.1
  31.0 1.3 pad_maximum_fusion
  32.4 2.1 pad_maximum_fusion.3
  34.5 1.9 pad_maximum_fusion.2
  36.5 0.2 all-gather.6.cloned.1.call-start
  36.7 0.9 pad_maximum_fusion.1
  37.7 0.1 convert_reduce_fusion
  37.9 0.1 copy.25
  38.0 0.8 sort.77
  39.0 1.7 gather_fusion.8
  40.7 0.2 convert_reduce_fusion.1
  41.0 0.6 gather_fusion.9
  41.7 0.7 reshape.128.ids_ref
  42.4 0.1 copy.21
  42.5 0.8 sort.76
  43.5 1.7 gather_fusion.6
  45.3 0.6 gather_fusion.7
  46.0 0.7 reshape.127.ids_ref
  46.8 0.8 sort.75
  47.8 1.7 gather_fusion.4
  49.6 0.6 gather_fusion.5
  50.3 0.6 reshape.126.ids_ref
  51.0 0.1 copy.13
  51.1 0.8 sort.74
  52.0 1.7 gather_fusion.2
  53.8 0.6 gather_fusion.3
  54.6 0.6 reshape.125.ids_ref
  55.3 0.8 sort.73
  56.3 1.7 gather_fusion
  58.0 0.6 gather_fusion.1
  58.8 0.6 reshape.124.ids_ref
  59.4 2.0 fusion.6.q_ref
  61.5 35.0 %all-gather.14.cloned.1.call-done.refs_0_.refs_1_ = bf16[2,2048,768]{2,1,0:T(8,128)(2,1)} async-done(((bf16[2,256,768]{2,1,0:T(8,128)(2,1)}), bf16[2,2048,768]{2,1,0:T(8,128)(2,1)}) %all-gather.14.cloned.1.call-update) | async-done | bytes 6291472 | tf_op jit(solution)/shard_map/all_gather | solution.py:204
  96.5 45.8 %shard_map.64 = (f32[6,768,256]{2,1,0:T(8,128)}, f32[6,2,6,1,256]{4,3,2,1,0:T(1,128)}) custom-call(s32[162]{0:T(256)} %reshape.128.ids_ref, s32[6]{0:T(128)} %copy-done.7, bf16[768,1536]{1,0:T(8,128)(2,1)} %fusion.6.q_ref, bf16[2,2048,768]{2,1,0:T(8,128)(2,1)} %all-gather.14.cloned.1.call-done.refs_0_.refs_1_, ...), custom_call_target="tpu_custom_call" | custom-call | tf_op jit(solution)/shard_map/pallas_call | solution.py:159
  142.3 70.7 %all-gather.12.cloned.1.call-done.refs_0_.refs_1_ = bf16[2,4096,768]{2,1,0:T(8,128)(2,1)} async-done(((bf16[2,512,768]{2,1,0:T(8,128)(2,1)}), bf16[2,4096,768]{2,1,0:T(8,128)(2,1)}) %all-gather.12.cloned.1.call-update) | async-done | bytes 12582928 | tf_op jit(solution)/shard_map/all_gather | solution.py:204
  213.0 87.7 %shard_map.65 = (f32[6,768,256]{2,1,0:T(8,128)}, f32[6,2,6,1,256]{4,3,2,1,0:T(1,128)}) custom-call(s32[162]{0:T(256)} %reshape.127.ids_ref, s32[6]{0:T(128)} %copy-done.6, bf16[768,1536]{1,0:T(8,128)(2,1)} %fusion.6.q_ref, bf16[2,4096,768]{2,1,0:T(8,128)(2,1)} %all-gather.12.cloned.1.call-done.refs_0_.refs_1_, ...), custom_call_target="tpu_custom_call" | custom-call | tf_op jit(solution)/shard_map/pallas_call | solution.py:159
  300.7 65.6 %shard_map.66 = (f32[6,768,256]{2,1,0:T(8,128)}, f32[6,2,6,1,256]{4,3,2,1,0:T(1,128)}) custom-call(s32[162]{0:T(256)} %reshape.126.ids_ref, s32[6]{0:T(128)} %copy-done.5, bf16[768,1536]{1,0:T(8,128)(2,1)} %fusion.6.q_ref, bf16[2,2048,768]{2,1,0:T(8,128)(2,1)} %all-gather.10.cloned.1.call-done.refs_0_.refs_1_, ...), custom_call_target="tpu_custom_call" | custom-call | tf_op jit(solution)/shard_map/pallas_call | solution.py:159
  366.3 49.3 %shard_map.67 = (f32[6,768,256]{2,1,0:T(8,128)}, f32[6,2,6,1,256]{4,3,2,1,0:T(1,128)}) custom-call(s32[162]{0:T(256)} %reshape.125.ids_ref, s32[6]{0:T(128)} %copy-done.4, bf16[768,1536]{1,0:T(8,128)(2,1)} %fusion.6.q_ref, bf16[2,2048,768]{2,1,0:T(8,128)(2,1)} %all-gather.8.cloned.1.call-done.refs_0_.refs_1_, ...), custom_call_target="tpu_custom_call" | custom-call | tf_op jit(solution)/shard_map/pallas_call | solution.py:159
  415.6 64.4 %shard_map.68 = bf16[1536,768]{1,0:T(8,128)(2,1)} custom-call(s32[162]{0:T(256)} %reshape.124.ids_ref, s32[6]{0:T(128)} %copy-done.3, bf16[768,1536]{1,0:T(8,128)(2,1)} %fusion.6.q_ref, bf16[2,2048,768]{2,1,0:T(8,128)(2,1)} %all-gather.6.cloned.1.call-done.refs_0_.refs_1_, bf16[2,2048,768]{2,1,0:T(8,128)(2,1)} %all-gather.6.cloned.1.call-done.refs_0_.refs_1_, ...), custom_call_target="tpu_custom_call" | custom-call | tf_op jit(solution)/shard_map/pallas_call | solution.py:159
  (88 shorter events, 2.3 us)
Async XLA Ops:
  6.5 16.2 %copy-start.8 = (f32[768]{0:T(1024)S(1)}, f32[768]{0:T(1024)}, u32[]{:S(2)}) copy-start(f32[768]{0:T(1024)} %param.14) | copy-start | bytes 9220
  6.5 90.0 %all-gather.14.cloned.1.call-start = ((), (), s32[]{:S(2)}) async-start(), calls=%async_computation.4 | async-start | bytes 7077888 | tf_op jit(solution)/shard_map/all_gather | solution.py:204
  22.7 3.9 copy-start.1
  25.1 1.4 copy-start
  28.6 184.4 %all-gather.12.cloned.1.call-start = ((), (), s32[]{:S(2)}) async-start(), calls=%async_computation.3 | async-start | bytes 14155776 | tf_op jit(solution)/shard_map/all_gather | solution.py:204
  32.3 5.4 %copy-start.2 = (s32[6,27]{1,0:T(8,128)S(1)}, s32[6,27]{1,0:T(8,128)}, u32[]{:S(2)}) copy-start(s32[6,27]{1,0:T(8,128)} %param.15) | copy-start | bytes 1948
  32.3 268.3 %all-gather.10.cloned.1.call-start = ((), (), s32[]{:S(2)}) async-start(), calls=%async_computation.2 | async-start | bytes 7077888 | tf_op jit(solution)/shard_map/all_gather | solution.py:204
  34.5 331.8 %all-gather.8.cloned.1.call-start = ((), (), s32[]{:S(2)}) async-start(), calls=%async_computation.1 | async-start | bytes 7077888 | tf_op jit(solution)/shard_map/all_gather | solution.py:204
  36.5 379.1 %all-gather.6.cloned.1.call-start = ((), (), s32[]{:S(2)}) async-start(), calls=%async_computation | async-start | bytes 7077888 | tf_op jit(solution)/shard_map/all_gather | solution.py:204
  37.8 7.3 %copy-start.7 = (s32[6]{0:T(128)}, s32[6]{0:T(128)S(1)}, u32[]{:S(2)}) copy-start(s32[6]{0:T(128)S(1)} %get-tuple-element.35.cnt_ref) | copy-start | bytes 76
  40.9 8.6 %copy-start.6 = (s32[6]{0:T(128)}, s32[6]{0:T(128)S(1)}, u32[]{:S(2)}) copy-start(s32[6]{0:T(128)S(1)} %get-tuple-element.38.cnt_ref) | copy-start | bytes 76
  40.9 9.4 %copy-start.5 = (s32[6]{0:T(128)}, s32[6]{0:T(128)S(1)}, u32[]{:S(2)}) copy-start(s32[6]{0:T(128)S(1)} %get-tuple-element.54.cnt_ref) | copy-start | bytes 76
  40.9 13.6 %copy-start.4 = (s32[6]{0:T(128)}, s32[6]{0:T(128)S(1)}, u32[]{:S(2)}) copy-start(s32[6]{0:T(128)S(1)} %get-tuple-element.56.cnt_ref) | copy-start | bytes 76
  40.9 17.8 %copy-start.3 = (s32[6]{0:T(128)}, s32[6]{0:T(128)S(1)}, u32[]{:S(2)}) copy-start(s32[6]{0:T(128)S(1)} %get-tuple-element.58.cnt_ref) | copy-start | bytes 76
  52.0 7.4 %copy-start.9 = (f32[768]{0:T(1024)S(1)}, f32[768]{0:T(1024)}, u32[]{:S(2)}) copy-start(f32[768]{0:T(1024)} %param.13) | copy-start | bytes 9220
Sparse Core Ops, SparseCore 0:
  28.7 67.7 all-gather.13
  98.1 114.8 all-gather.11
  214.6 63.5 all-gather.9
  279.6 63.3 all-gather.7
  344.5 63.4 all-gather.5
where the time goes:
time: 484 us; the launch traced here: 487 us
  Pallas kernels  313 us (65%)
  waiting for transfers between devices  106 us (22%)
  local copies, waits for them, and re-layouts  24.2 us (5%)
  other arithmetic  19.3 us (4%)
  between operations  13.4 us (3%)
  blocking collectives  10.6 us (2%)
    pallas_call x5, Pallas kernels, window_attention(): pl.pallas_call(functools.partial(attention_kernel, first=first, last=last...  313 us
    all_gather x5, waiting for transfers between devices, on_device(): extended = lax.all_gather(paired, 'tok', axis=1, tiled=True)  106 us
    psum x1, blocking collectives, on_device(): lax.psum((square_sums(query_states), square_sums(key_states)), 'head')  10.6 us
  transfers between devices with their start and end apart: 5, of which 2 were waited for; matrix products, arithmetic and copies ran while one was open for 7% of the time, Pallas kernels for 51%

commit v1 on v0

--- a/solution.py
+++ b/solution.py
@@ -12,6 +12,9 @@
 MODEL_DIM = 3072
 TILE_TOKENS = 256
 WINDOW_SLOTS = 27
+FRAME_SLOTS = 9
+FRAME_ROWS = 4
+FRAME_COLS = 4
 SLOTS_PER_STEP = 1
 STATS_HALF = 64
 
@@ -112,11 +115,11 @@
             stats_out[0, 1] = l_sc[...]
 
 
-def window_attention(query_t, paired, ids, counts, state, last):
+def window_attention(query_t, paired, ids, counts, state, last, bound):
     width, rows = query_t.shape
     local_tiles = rows // TILE_TOKENS
     heads = width // HEAD_DIM
-    steps = WINDOW_SLOTS // SLOTS_PER_STEP
+    steps = bound // SLOTS_PER_STEP
     first = state is None
 
     def window_spec(lead, sub):
@@ -181,6 +184,26 @@
     return ids.reshape(-1).astype(jnp.int32), counts.astype(jnp.int32)
 
 
+def phase_bound(local_tiles, tile_count, start, size):
+    per_frame = FRAME_ROWS * FRAME_COLS
+    frames = tile_count // per_frame
+    best = 0
+    for i in range(tile_count):
+        fi, ri, ci = i // per_frame, i // FRAME_COLS % FRAME_ROWS, i % FRAME_COLS
+        total = 0
+        for fj in (fi - 1, fi, fi + 1):
+            if not 0 <= fj < frames:
+                continue
+            near = 0
+            for j in range(fj * per_frame, (fj + 1) * per_frame):
+                rj, cj = j // FRAME_COLS % FRAME_ROWS, j % FRAME_COLS
+                if abs(ri - rj) <= 2 and abs(ci - cj) <= 2 and start <= j % local_tiles < start + size:
+                    near += 1
+            total += min(FRAME_SLOTS, near)
+        best = max(best, total)
+    return max(1, min(WINDOW_SLOTS, best))
+
+
 def phase_sizes(local_tiles):
     if local_tiles >= 3:
         return [1, 2] + [1] * (local_tiles - 3)
@@ -203,8 +226,9 @@
         paired = jnp.stack([sent_keys[part], value_states[part]])
         extended = lax.all_gather(paired, "tok", axis=1, tiled=True)
         ids, counts = phase_windows(windows, local_tiles, start, size, tile_count)
+        bound = phase_bound(local_tiles, tile_count, start, size)
         state = window_attention(
-            query_t, extended, ids, counts, state, number == len(sizes) - 1
+            query_t, extended, ids, counts, state, number == len(sizes) - 1, bound
         )
         start += size
     return state

time: 484 us -> 471 us (0.973); the launches traced: 487 us -> 466 us
  Pallas kernels: 313 us -> 280 us
  waiting for transfers between devices: 106 us -> 118 us
    pallas_call x5, Pallas kernels: 313 us -> 280 us  [window_attention(): pl.pallas_call(functools.partial(attention_kernel, first=first, last=last...]
    all_gather x5, waiting for transfers between devices: 106 us -> 118 us  [on_device(): extended = lax.all_gather(paired, 'tok', axis=1, tiled=True)]
  transfers between devices with their start and end apart: 5 -> 5, of which waited for: 2 -> 3; matrix products, arithmetic and copies ran while one was open for 7% -> 7% of each run, Pallas kernels for 51% -> 49%
where the time goes in v1:
time: 471 us; the launch traced here: 466 us
  Pallas kernels  280 us (59%)
  waiting for transfers between devices  118 us (25%)
  local copies, waits for them, and re-layouts  24.2 us (5%)
  other arithmetic  19.3 us (4%)
  between operations  13.4 us (3%)
  blocking collectives  10.6 us (2%)
    pallas_call x5, Pallas kernels, window_attention(): pl.pallas_call(functools.partial(attention_kernel, first=first, last=last...  280 us
    all_gather x5, waiting for transfers between devices, on_device(): extended = lax.all_gather(paired, 'tok', axis=1, tiled=True)  118 us
    psum x1, blocking collectives, on_device(): lax.psum((square_sums(query_states), square_sums(key_states)), 'head')  10.6 us
  transfers between devices with their start and end apart: 5, of which 3 were waited for; matrix products, arithmetic and copies ran while one was open for 7% of the time, Pallas kernels for 49%

profile of v1, /device:TPU:11, one launch (start us, length us, event | category | flops | bytes accessed | tf_op | source)
XLA Modules:
  0.0 466.4 jit_solution(9770484815971046152)
XLA Ops:
  6.5 2.8 copy.12
  9.4 0.5 fusion
  9.9 2.2 fusion.3
  12.1 10.6 %all-reduce = (f32[1536]{0:T(1024)S(1)}, f32[1536]{0:T(1024)S(1)}) all-reduce(f32[1536]{0:T(1024)S(1)} %fusion, f32[1536]{0:T(1024)S(1)} %fusion.3), channel_id=1, replica_groups=mesh['tok'=8,'head'=4] {'head'}, use_global_device_ids=true, to_apply=%region_3.6 | all-reduce | flops 3072 | bytes 24576 | tf_op jit(solution)/shard_map/psum | solution.py:218
  22.7 2.4 fusion.5
  25.1 1.4 copy-done
  26.5 1.1 slice_bitcast_fusion.2
  27.6 1.0 pad_maximum_fusion.4
  28.7 1.2 slice_bitcast_fusion
  29.8 1.2 slice_bitcast_fusion.1
  31.0 1.3 pad_maximum_fusion
  32.4 2.1 pad_maximum_fusion.3
  34.5 1.9 pad_maximum_fusion.2
  36.5 0.2 all-gather.6.cloned.1.call-start
  36.7 0.9 pad_maximum_fusion.1
  37.7 0.1 convert_reduce_fusion
  38.0 0.8 sort.77
  39.0 1.7 gather_fusion.8
  40.7 0.2 convert_reduce_fusion.1
  41.0 0.6 gather_fusion.9
  41.7 0.7 reshape.128.ids_ref
  42.4 0.1 copy.21
  42.5 0.8 sort.76
  43.5 1.7 gather_fusion.6
  45.3 0.6 gather_fusion.7
  46.0 0.7 reshape.127.ids_ref
  46.8 0.8 sort.75
  47.8 1.7 gather_fusion.4
  49.6 0.6 gather_fusion.5
  50.3 0.6 reshape.126.ids_ref
  51.0 0.1 copy.13
  51.1 0.8 sort.74
  52.0 1.7 gather_fusion.2
  53.8 0.6 gather_fusion.3
  54.6 0.6 reshape.125.ids_ref
  55.3 0.8 sort.73
  56.3 1.7 gather_fusion
  58.0 0.6 gather_fusion.1
  58.8 0.6 reshape.124.ids_ref
  59.4 2.0 fusion.6.q_ref
  61.5 35.0 %all-gather.14.cloned.1.call-done.refs_0_.refs_1_ = bf16[2,2048,768]{2,1,0:T(8,128)(2,1)} async-done(((bf16[2,256,768]{2,1,0:T(8,128)(2,1)}), bf16[2,2048,768]{2,1,0:T(8,128)(2,1)}) %all-gather.14.cloned.1.call-update) | async-done | bytes 6291472 | tf_op jit(solution)/shard_map/all_gather | solution.py:227
  96.5 43.1 %shard_map.64 = (f32[6,768,256]{2,1,0:T(8,128)}, f32[6,2,6,1,256]{4,3,2,1,0:T(1,128)}) custom-call(s32[162]{0:T(256)} %reshape.128.ids_ref, s32[6]{0:T(128)} %copy-done.7, bf16[768,1536]{1,0:T(8,128)(2,1)} %fusion.6.q_ref, bf16[2,2048,768]{2,1,0:T(8,128)(2,1)} %all-gather.14.cloned.1.call-done.refs_0_.refs_1_, ...), custom_call_target="tpu_custom_call" | custom-call | tf_op jit(solution)/shard_map/pallas_call | solution.py:162
  139.6 73.4 %all-gather.12.cloned.1.call-done.refs_0_.refs_1_ = bf16[2,4096,768]{2,1,0:T(8,128)(2,1)} async-done(((bf16[2,512,768]{2,1,0:T(8,128)(2,1)}), bf16[2,4096,768]{2,1,0:T(8,128)(2,1)}) %all-gather.12.cloned.1.call-update) | async-done | bytes 12582928 | tf_op jit(solution)/shard_map/all_gather | solution.py:227
  213.0 86.8 %shard_map.65 = (f32[6,768,256]{2,1,0:T(8,128)}, f32[6,2,6,1,256]{4,3,2,1,0:T(1,128)}) custom-call(s32[162]{0:T(256)} %reshape.127.ids_ref, s32[6]{0:T(128)} %copy-done.6, bf16[768,1536]{1,0:T(8,128)(2,1)} %fusion.6.q_ref, bf16[2,4096,768]{2,1,0:T(8,128)(2,1)} %all-gather.12.cloned.1.call-done.refs_0_.refs_1_, ...), custom_call_target="tpu_custom_call" | custom-call | tf_op jit(solution)/shard_map/pallas_call | solution.py:162
  299.8 52.8 %shard_map.66 = (f32[6,768,256]{2,1,0:T(8,128)}, f32[6,2,6,1,256]{4,3,2,1,0:T(1,128)}) custom-call(s32[162]{0:T(256)} %reshape.126.ids_ref, s32[6]{0:T(128)} %copy-done.5, bf16[768,1536]{1,0:T(8,128)(2,1)} %fusion.6.q_ref, bf16[2,2048,768]{2,1,0:T(8,128)(2,1)} %all-gather.10.cloned.1.call-done.refs_0_.refs_1_, ...), custom_call_target="tpu_custom_call" | custom-call | tf_op jit(solution)/shard_map/pallas_call | solution.py:162
  352.6 45.5 %shard_map.67 = (f32[6,768,256]{2,1,0:T(8,128)}, f32[6,2,6,1,256]{4,3,2,1,0:T(1,128)}) custom-call(s32[162]{0:T(256)} %reshape.125.ids_ref, s32[6]{0:T(128)} %copy-done.4, bf16[768,1536]{1,0:T(8,128)(2,1)} %fusion.6.q_ref, bf16[2,2048,768]{2,1,0:T(8,128)(2,1)} %all-gather.8.cloned.1.call-done.refs_0_.refs_1_, ...), custom_call_target="tpu_custom_call" | custom-call | tf_op jit(solution)/shard_map/pallas_call | solution.py:162
  398.0 9.9 %all-gather.6.cloned.1.call-done.refs_0_.refs_1_ = bf16[2,2048,768]{2,1,0:T(8,128)(2,1)} async-done(((bf16[2,256,768]{2,1,0:T(8,128)(2,1)}), bf16[2,2048,768]{2,1,0:T(8,128)(2,1)}) %all-gather.6.cloned.1.call-update) | async-done | bytes 6291472 | tf_op jit(solution)/shard_map/all_gather | solution.py:227
  408.0 51.9 %shard_map.68 = bf16[1536,768]{1,0:T(8,128)(2,1)} custom-call(s32[162]{0:T(256)} %reshape.124.ids_ref, s32[6]{0:T(128)} %copy-done.3, bf16[768,1536]{1,0:T(8,128)(2,1)} %fusion.6.q_ref, bf16[2,2048,768]{2,1,0:T(8,128)(2,1)} %all-gather.6.cloned.1.call-done.refs_0_.refs_1_, bf16[2,2048,768]{2,1,0:T(8,128)(2,1)} %all-gather.6.cloned.1.call-done.refs_0_.refs_1_, ...), custom_call_target="tpu_custom_call" | custom-call | tf_op jit(solution)/shard_map/pallas_call | solution.py:162
  (88 shorter events, 2.4 us)
Async XLA Ops:
  6.5 16.2 %copy-start.8 = (f32[768]{0:T(1024)S(1)}, f32[768]{0:T(1024)}, u32[]{:S(2)}) copy-start(f32[768]{0:T(1024)} %param.14) | copy-start | bytes 9220
  6.5 90.0 %all-gather.14.cloned.1.call-start = ((), (), s32[]{:S(2)}) async-start(), calls=%async_computation.4 | async-start | bytes 7077888 | tf_op jit(solution)/shard_map/all_gather | solution.py:227
  22.7 3.9 copy-start.1
  25.1 1.4 copy-start
  28.6 184.4 %all-gather.12.cloned.1.call-start = ((), (), s32[]{:S(2)}) async-start(), calls=%async_computation.3 | async-start | bytes 14155776 | tf_op jit(solution)/shard_map/all_gather | solution.py:227
  32.3 5.4 %copy-start.2 = (s32[6,27]{1,0:T(8,128)S(1)}, s32[6,27]{1,0:T(8,128)}, u32[]{:S(2)}) copy-start(s32[6,27]{1,0:T(8,128)} %param.15) | copy-start | bytes 1948
  32.3 267.5 %all-gather.10.cloned.1.call-start = ((), (), s32[]{:S(2)}) async-start(), calls=%async_computation.2 | async-start | bytes 7077888 | tf_op jit(solution)/shard_map/all_gather | solution.py:227
  34.5 318.1 %all-gather.8.cloned.1.call-start = ((), (), s32[]{:S(2)}) async-start(), calls=%async_computation.1 | async-start | bytes 7077888 | tf_op jit(solution)/shard_map/all_gather | solution.py:227
  36.5 371.5 %all-gather.6.cloned.1.call-start = ((), (), s32[]{:S(2)}) async-start(), calls=%async_computation | async-start | bytes 7077888 | tf_op jit(solution)/shard_map/all_gather | solution.py:227
  37.8 7.3 %copy-start.7 = (s32[6]{0:T(128)}, s32[6]{0:T(128)S(1)}, u32[]{:S(2)}) copy-start(s32[6]{0:T(128)S(1)} %get-tuple-element.35.cnt_ref) | copy-start | bytes 76
  40.9 8.6 %copy-start.6 = (s32[6]{0:T(128)}, s32[6]{0:T(128)S(1)}, u32[]{:S(2)}) copy-start(s32[6]{0:T(128)S(1)} %get-tuple-element.38.cnt_ref) | copy-start | bytes 76
  40.9 9.4 %copy-start.5 = (s32[6]{0:T(128)}, s32[6]{0:T(128)S(1)}, u32[]{:S(2)}) copy-start(s32[6]{0:T(128)S(1)} %get-tuple-element.54.cnt_ref) | copy-start | bytes 76
  40.9 13.6 %copy-start.4 = (s32[6]{0:T(128)}, s32[6]{0:T(128)S(1)}, u32[]{:S(2)}) copy-start(s32[6]{0:T(128)S(1)} %get-tuple-element.56.cnt_ref) | copy-start | bytes 76
  40.9 17.8 %copy-start.3 = (s32[6]{0:T(128)}, s32[6]{0:T(128)S(1)}, u32[]{:S(2)}) copy-start(s32[6]{0:T(128)S(1)} %get-tuple-element.58.cnt_ref) | copy-start | bytes 76
  52.0 7.4 %copy-start.9 = (f32[768]{0:T(1024)S(1)}, f32[768]{0:T(1024)}, u32[]{:S(2)}) copy-start(f32[768]{0:T(1024)} %param.13) | copy-start | bytes 9220
Sparse Core Ops, SparseCore 0:
  28.7 67.7 all-gather.13
  98.1 114.8 all-gather.11
  214.6 63.5 all-gather.9
  279.6 63.3 all-gather.7
  344.5 63.4 all-gather.5

commit v2 on v1

--- a/solution.py
+++ b/solution.py
@@ -210,12 +210,25 @@
     return [local_tiles]
 
 
-def on_device(query_states, key_states, value_states, query_gain, key_gain, windows, tok_count):
+def head_sums(partial, head_count):
+    if head_count & (head_count - 1):
+        return lax.psum(partial, "head")
+    step = 1
+    while step < head_count:
+        pairs = [(i, i ^ step) for i in range(head_count)]
+        partial = partial + lax.ppermute(partial, "head", pairs)
+        step *= 2
+    return partial
+
+
+def on_device(query_states, key_states, value_states, query_gain, key_gain, windows, tok_count, head_count):
     rows = query_states.shape[0]
     local_tiles = rows // TILE_TOKENS
     tile_count = tok_count * local_tiles
     sizes = phase_sizes(local_tiles)
-    query_total, key_total = lax.psum((square_sums(query_states), square_sums(key_states)), "head")
+    query_total, key_total = head_sums(
+        jnp.stack([square_sums(query_states), square_sums(key_states)]), head_count
+    )
     query_normed = normalize_rows(query_states, query_total, query_gain)
     sent_keys = normalize_rows(key_states, key_total, key_gain)
     query_t = query_normed.T
@@ -245,7 +258,9 @@
     )
     out_specs = P("tok", "head")
     return jax.shard_map(
-        functools.partial(on_device, tok_count=mesh.shape["tok"]),
+        functools.partial(
+            on_device, tok_count=mesh.shape["tok"], head_count=mesh.shape["head"]
+        ),
         mesh=mesh,
         in_specs=in_specs,
         out_specs=out_specs,

time: 471 us -> 465 us (0.987)
  Pallas kernels: 280 us -> 297 us
  blocking collectives: 10.6 us -> 0 us
  waiting for transfers between devices: 118 us -> 108 us
    pallas_call x5, Pallas kernels: 280 us -> 297 us  [window_attention(): pl.pallas_call(functools.partial(attention_kernel, first=first, last=last...]
    all_gather x5, waiting for transfers between devices: 118 us -> 105 us  [on_device(): extended = lax.all_gather(paired, 'tok', axis=1, tiled=True)]
    psum x1 -> x0, blocking collectives: 10.6 us -> none  [on_device(): lax.psum((square_sums(query_states), square_sums(key_states)), 'head')]
  transfers between devices with their start and end apart: 5 -> 7, of which waited for: 3 -> 4; matrix products, arithmetic and copies ran while one was open for 7% -> 7% of each run, Pallas kernels for 49% -> 52%
where the time goes in v2:
time: 465 us; the launch traced here: 463 us
  Pallas kernels  297 us (64%)
  waiting for transfers between devices  108 us (23%)
  local copies, waits for them, and re-layouts  24.2 us (5%)
  other arithmetic  17.9 us (4%)
  between operations  13.5 us (3%)
    pallas_call x5, Pallas kernels, window_attention(): pl.pallas_call(functools.partial(attention_kernel, first=first, last=last...  297 us
    all_gather x5, waiting for transfers between devices, on_device(): extended = lax.all_gather(paired, 'tok', axis=1, tiled=True)  105 us
  transfers between devices with their start and end apart: 7, of which 4 were waited for; matrix products, arithmetic and copies ran while one was open for 7% of the time, Pallas kernels for 52%

profile of v2, /device:TPU:11, one launch (start us, length us, event | category | flops | bytes accessed | tf_op | source)
XLA Modules:
  0.0 463.5 jit_solution(17861354895105238)
XLA Ops:
  6.5 2.8 copy.12
  9.4 0.5 fusion
  9.9 2.5 fusion.3
  12.4 0.3 collective-permute-start
  12.8 2.3 collective-permute-done
  15.1 1.3 collective-permute-start.1
  16.4 1.3 collective-permute-done.1
  17.8 0.6 fusion.5
  18.4 1.4 copy-done.1
  19.8 1.1 slice_bitcast_fusion.2
  20.9 1.0 pad_maximum_fusion.4
  21.9 1.2 slice_bitcast_fusion.1
  23.1 1.2 slice_bitcast_fusion
  24.3 1.3 pad_maximum_fusion
  25.7 2.1 pad_maximum_fusion.3
  27.8 1.9 pad_maximum_fusion.2
  29.8 0.2 all-gather.6.cloned.1.call-start
  30.0 0.9 pad_maximum_fusion.1
  31.0 0.1 convert_reduce_fusion
  31.2 0.8 sort.77
  32.2 1.7 gather_fusion.8
  34.0 0.2 convert_reduce_fusion.1
  34.3 0.6 gather_fusion.9
  35.0 0.7 reshape.152.ids_ref
  35.8 0.8 sort.76
  36.8 1.7 gather_fusion.6
  38.6 0.6 gather_fusion.7
  39.3 0.7 reshape.151.ids_ref
  40.1 0.8 sort.75
  41.1 1.7 gather_fusion.4
  42.9 0.6 gather_fusion.5
  43.6 0.6 reshape.150.ids_ref
  44.3 0.8 sort.74
  45.3 1.7 gather_fusion.2
  47.1 0.6 gather_fusion.3
  47.8 0.6 reshape.149.ids_ref
  48.5 0.8 sort.73
  49.5 1.7 gather_fusion
  51.3 0.6 gather_fusion.1
  52.1 0.6 reshape.148.ids_ref
  52.7 2.0 fusion.6.q_ref
  54.7 33.8 %all-gather.14.cloned.1.call-done.refs_0_.refs_1_ = bf16[2,2048,768]{2,1,0:T(8,128)(2,1)} async-done(((bf16[2,256,768]{2,1,0:T(8,128)(2,1)}), bf16[2,2048,768]{2,1,0:T(8,128)(2,1)}) %all-gather.14.cloned.1.call-update) | async-done | bytes 6291472 | tf_op jit(solution)/shard_map/all_gather | solution.py:240
  88.5 45.4 %shard_map.64 = (f32[6,768,256]{2,1,0:T(8,128)}, f32[6,2,6,1,256]{4,3,2,1,0:T(1,128)}) custom-call(s32[162]{0:T(256)} %reshape.152.ids_ref, s32[6]{0:T(128)} %copy-done.8, bf16[768,1536]{1,0:T(8,128)(2,1)} %fusion.6.q_ref, bf16[2,2048,768]{2,1,0:T(8,128)(2,1)} %all-gather.14.cloned.1.call-done.refs_0_.refs_1_, ...), custom_call_target="tpu_custom_call" | custom-call | tf_op jit(solution)/shard_map/pallas_call | solution.py:162
  133.9 71.0 %all-gather.12.cloned.1.call-done.refs_0_.refs_1_ = bf16[2,4096,768]{2,1,0:T(8,128)(2,1)} async-done(((bf16[2,512,768]{2,1,0:T(8,128)(2,1)}), bf16[2,4096,768]{2,1,0:T(8,128)(2,1)}) %all-gather.12.cloned.1.call-update) | async-done | bytes 12582928 | tf_op jit(solution)/shard_map/all_gather | solution.py:240
  204.9 92.3 %shard_map.65 = (f32[6,768,256]{2,1,0:T(8,128)}, f32[6,2,6,1,256]{4,3,2,1,0:T(1,128)}) custom-call(s32[162]{0:T(256)} %reshape.151.ids_ref, s32[6]{0:T(128)} %copy-done.7, bf16[768,1536]{1,0:T(8,128)(2,1)} %fusion.6.q_ref, bf16[2,4096,768]{2,1,0:T(8,128)(2,1)} %all-gather.12.cloned.1.call-done.refs_0_.refs_1_, ...), custom_call_target="tpu_custom_call" | custom-call | tf_op jit(solution)/shard_map/pallas_call | solution.py:162
  297.2 56.6 %shard_map.66 = (f32[6,768,256]{2,1,0:T(8,128)}, f32[6,2,6,1,256]{4,3,2,1,0:T(1,128)}) custom-call(s32[162]{0:T(256)} %reshape.150.ids_ref, s32[6]{0:T(128)} %copy-done.6, bf16[768,1536]{1,0:T(8,128)(2,1)} %fusion.6.q_ref, bf16[2,2048,768]{2,1,0:T(8,128)(2,1)} %all-gather.10.cloned.1.call-done.refs_0_.refs_1_, ...), custom_call_target="tpu_custom_call" | custom-call | tf_op jit(solution)/shard_map/pallas_call | solution.py:162
  353.8 47.5 %shard_map.67 = (f32[6,768,256]{2,1,0:T(8,128)}, f32[6,2,6,1,256]{4,3,2,1,0:T(1,128)}) custom-call(s32[162]{0:T(256)} %reshape.149.ids_ref, s32[6]{0:T(128)} %copy-done.5, bf16[768,1536]{1,0:T(8,128)(2,1)} %fusion.6.q_ref, bf16[2,2048,768]{2,1,0:T(8,128)(2,1)} %all-gather.8.cloned.1.call-done.refs_0_.refs_1_, ...), custom_call_target="tpu_custom_call" | custom-call | tf_op jit(solution)/shard_map/pallas_call | solution.py:162
  401.3 55.6 %shard_map.68 = bf16[1536,768]{1,0:T(8,128)(2,1)} custom-call(s32[162]{0:T(256)} %reshape.148.ids_ref, s32[6]{0:T(128)} %copy-done.4, bf16[768,1536]{1,0:T(8,128)(2,1)} %fusion.6.q_ref, bf16[2,2048,768]{2,1,0:T(8,128)(2,1)} %all-gather.6.cloned.1.call-done.refs_0_.refs_1_, bf16[2,2048,768]{2,1,0:T(8,128)(2,1)} %all-gather.6.cloned.1.call-done.refs_0_.refs_1_, ...), custom_call_target="tpu_custom_call" | custom-call | tf_op jit(solution)/shard_map/pallas_call | solution.py:162
  (97 shorter events, 2.7 us)
Async XLA Ops:
  6.5 11.2 %copy-start.9 = (f32[768]{0:T(1024)S(1)}, f32[768]{0:T(1024)}, u32[]{:S(2)}) copy-start(f32[768]{0:T(1024)} %param.14) | copy-start | bytes 9220
  6.5 82.0 %all-gather.14.cloned.1.call-start = ((), (), s32[]{:S(2)}) async-start(), calls=%async_computation.4 | async-start | bytes 7077888 | tf_op jit(solution)/shard_map/all_gather | solution.py:240
  9.4 8.4 %copy-start = (bf16[1536,768]{1,0:T(8,128)(2,1)S(1)}, bf16[1536,768]{1,0:T(8,128)(2,1)}, u32[]{:S(2)}) copy-start(bf16[1536,768]{1,0:T(8,128)(2,1)} %param.11) | copy-start | bytes 7077892
  9.4 10.4 %copy-start.2 = (bf16[1536,768]{1,0:T(8,128)(2,1)S(1)}, bf16[1536,768]{1,0:T(8,128)(2,1)}, u32[]{:S(2)}) copy-start(bf16[1536,768]{1,0:T(8,128)(2,1)} %param.12) | copy-start | bytes 7077892
  12.4 2.6 collective-permute-start
  15.1 2.6 collective-permute-start.1
  18.4 1.4 copy-start.1
  21.9 183.0 %all-gather.12.cloned.1.call-start = ((), (), s32[]{:S(2)}) async-start(), calls=%async_computation.3 | async-start | bytes 14155776 | tf_op jit(solution)/shard_map/all_gather | solution.py:240
  25.6 5.4 %copy-start.3 = (s32[6,27]{1,0:T(8,128)S(1)}, s32[6,27]{1,0:T(8,128)}, u32[]{:S(2)}) copy-start(s32[6,27]{1,0:T(8,128)} %param.15) | copy-start | bytes 1948
  25.6 271.6 %all-gather.10.cloned.1.call-start = ((), (), s32[]{:S(2)}) async-start(), calls=%async_computation.2 | async-start | bytes 7077888 | tf_op jit(solution)/shard_map/all_gather | solution.py:240
  27.8 326.1 %all-gather.8.cloned.1.call-start = ((), (), s32[]{:S(2)}) async-start(), calls=%async_computation.1 | async-start | bytes 7077888 | tf_op jit(solution)/shard_map/all_gather | solution.py:240
  29.8 371.6 %all-gather.6.cloned.1.call-start = ((), (), s32[]{:S(2)}) async-start(), calls=%async_computation | async-start | bytes 7077888 | tf_op jit(solution)/shard_map/all_gather | solution.py:240
  31.1 7.3 %copy-start.8 = (s32[6]{0:T(128)}, s32[6]{0:T(128)S(1)}, u32[]{:S(2)}) copy-start(s32[6]{0:T(128)S(1)} %get-tuple-element.35.cnt_ref) | copy-start | bytes 76
  34.1 8.6 %copy-start.7 = (s32[6]{0:T(128)}, s32[6]{0:T(128)S(1)}, u32[]{:S(2)}) copy-start(s32[6]{0:T(128)S(1)} %get-tuple-element.38.cnt_ref) | copy-start | bytes 76
  34.1 9.4 %copy-start.6 = (s32[6]{0:T(128)}, s32[6]{0:T(128)S(1)}, u32[]{:S(2)}) copy-start(s32[6]{0:T(128)S(1)} %get-tuple-element.54.cnt_ref) | copy-start | bytes 76
  34.2 13.6 %copy-start.5 = (s32[6]{0:T(128)}, s32[6]{0:T(128)S(1)}, u32[]{:S(2)}) copy-start(s32[6]{0:T(128)S(1)} %get-tuple-element.56.cnt_ref) | copy-start | bytes 76
  34.2 17.8 %copy-start.4 = (s32[6]{0:T(128)}, s32[6]{0:T(128)S(1)}, u32[]{:S(2)}) copy-start(s32[6]{0:T(128)S(1)} %get-tuple-element.58.cnt_ref) | copy-start | bytes 76
  45.3 7.4 %copy-start.10 = (f32[768]{0:T(1024)S(1)}, f32[768]{0:T(1024)}, u32[]{:S(2)}) copy-start(f32[768]{0:T(1024)} %param.13) | copy-start | bytes 9220
Sparse Core Ops, SparseCore 0:
  22.0 66.4 all-gather.13
  90.1 114.7 all-gather.11
  206.5 63.5 all-gather.9
  271.5 63.4 all-gather.7
  336.5 63.4 all-gather.5

commit v3 on v2

--- a/solution.py
+++ b/solution.py
@@ -169,22 +169,29 @@
     )(*operands)
 
 
-def phase_windows(windows, local_tiles, start, size, tile_count):
+def phase_windows(windows, local_tiles, start, size, tile_count, shard, local):
     safe = jnp.clip(windows, 0, tile_count - 1)
     position = safe % local_tiles
-    inside = (windows >= 0) & (position >= start) & (position < start + size)
-    block = (safe // local_tiles) * size + jnp.clip(position - start, 0, size - 1)
+    own = safe // local_tiles == shard
+    if local:
+        inside = (windows >= 0) & own
+        block = position
+        blocks = local_tiles
+    else:
+        inside = (windows >= 0) & (position >= start) & (position < start + size) & ~own
+        block = (safe // local_tiles) * size + jnp.clip(position - start, 0, size - 1)
+        blocks = (tile_count // local_tiles) * size
     order = jnp.argsort(jnp.logical_not(inside).astype(jnp.int32), axis=1, stable=True)
     ids = jnp.take_along_axis(block, order, axis=1)
     counts = jnp.sum(inside.astype(jnp.int32), axis=1)
     last = jnp.take_along_axis(ids, jnp.maximum(counts - 1, 0)[:, None], axis=1)
     slot = lax.broadcasted_iota(jnp.int32, ids.shape, 1)
     ids = jnp.where(slot < counts[:, None], ids, last)
-    ids = jnp.clip(ids, 0, (tile_count // local_tiles) * size - 1)
+    ids = jnp.clip(ids, 0, blocks - 1)
     return ids.reshape(-1).astype(jnp.int32), counts.astype(jnp.int32)
 
 
-def phase_bound(local_tiles, tile_count, start, size):
+def phase_bound(local_tiles, tile_count, start, size, local=False):
     per_frame = FRAME_ROWS * FRAME_COLS
     frames = tile_count // per_frame
     best = 0
@@ -197,7 +204,11 @@
             near = 0
             for j in range(fj * per_frame, (fj + 1) * per_frame):
                 rj, cj = j // FRAME_COLS % FRAME_ROWS, j % FRAME_COLS
-                if abs(ri - rj) <= 2 and abs(ci - cj) <= 2 and start <= j % local_tiles < start + size:
+                if local:
+                    chosen = j // local_tiles == i // local_tiles
+                else:
+                    chosen = start <= j % local_tiles < start + size
+                if abs(ri - rj) <= 2 and abs(ci - cj) <= 2 and chosen:
                     near += 1
             total += min(FRAME_SLOTS, near)
         best = max(best, total)
@@ -232,13 +243,17 @@
     query_normed = normalize_rows(query_states, query_total, query_gain)
     sent_keys = normalize_rows(key_states, key_total, key_gain)
     query_t = query_normed.T
-    state = None
+    shard = lax.axis_index("tok")
+    own = jnp.stack([sent_keys, value_states])
+    ids, counts = phase_windows(windows, local_tiles, 0, local_tiles, tile_count, shard, True)
+    bound = phase_bound(local_tiles, tile_count, 0, local_tiles, local=True)
+    state = window_attention(query_t, own, ids, counts, None, False, bound)
     start = 0
     for number, size in enumerate(sizes):
         part = slice(start * TILE_TOKENS, (start + size) * TILE_TOKENS)
         paired = jnp.stack([sent_keys[part], value_states[part]])
         extended = lax.all_gather(paired, "tok", axis=1, tiled=True)
-        ids, counts = phase_windows(windows, local_tiles, start, size, tile_count)
+        ids, counts = phase_windows(windows, local_tiles, start, size, tile_count, shard, False)
         bound = phase_bound(local_tiles, tile_count, start, size)
         state = window_attention(
             query_t, extended, ids, counts, state, number == len(sizes) - 1, bound

time: 465 us -> 453 us (0.974)
  Pallas kernels: 297 us -> 262 us
  waiting for transfers between devices: 108 us -> 117 us
  local copies, waits for them, and re-layouts: 24.2 us -> 29.7 us
  other arithmetic: 17.9 us -> 23.3 us
    pallas_call x5 -> x6, Pallas kernels: 297 us -> 262 us  [window_attention(): pl.pallas_call(functools.partial(attention_kernel, first=first, last=last...]
    all_gather x5, waiting for transfers between devices: 105 us -> 114 us  [on_device(): extended = lax.all_gather(paired, 'tok', axis=1, tiled=True)]
    gather x15 -> x18, local copies, waits for them, and re-layouts: 9.09 us -> 11.1 us  [phase_windows(): ids = jnp.take_along_axis(block, order, axis=1)]
  transfers between devices with their start and end apart: 7 -> 7, of which waited for: 4 -> 5; matrix products, arithmetic and copies ran while one was open for 7% -> 9% of each run, Pallas kernels for 52% -> 50%
where the time goes in v3:
time: 453 us; the launch traced here: 448 us
  Pallas kernels  262 us (58%)
  waiting for transfers between devices  117 us (26%)
  local copies, waits for them, and re-layouts  29.7 us (7%)
  other arithmetic  23.3 us (5%)
  between operations  13.5 us (3%)
    pallas_call x6, Pallas kernels, window_attention(): pl.pallas_call(functools.partial(attention_kernel, first=first, last=last...  262 us
    all_gather x5, waiting for transfers between devices, on_device(): extended = lax.all_gather(paired, 'tok', axis=1, tiled=True)  114 us
    gather x18, local copies, waits for them, and re-layouts, phase_windows(): ids = jnp.take_along_axis(block, order, axis=1)  11.1 us
  transfers between devices with their start and end apart: 7, of which 5 were waited for; matrix products, arithmetic and copies ran while one was open for 9% of the time, Pallas kernels for 50%

profile of v3, /device:TPU:11, one launch (start us, length us, event | category | flops | bytes accessed | tf_op | source)
XLA Modules:
  0.0 447.6 jit_solution(14968831859287876221)
XLA Ops:
  6.5 4.4 copy.12
  11.0 2.3 fusion
  14.2 2.3 collective-permute-done
  16.5 1.3 collective-permute-start.1
  17.8 1.3 collective-permute-done.1
  19.8 1.3 slice_bitcast_fusion.2
  21.6 1.0 pad_maximum_fusion.5
  22.7 1.2 slice_bitcast_fusion.1
  23.8 1.2 slice_bitcast_fusion
  25.0 1.3 pad_maximum_fusion.1
  26.5 2.1 pad_maximum_fusion.4
  28.6 2.0 pad_maximum_fusion.3
  30.6 1.0 pad_maximum_fusion.2
  31.6 0.8 convert_reduce_fusion
  32.6 0.8 sort.92
  33.6 0.9 convert_reduce_fusion.1
  34.5 1.8 gather_fusion.10
  37.3 0.7 reshape.171.ids_ref
  38.1 0.8 sort.91
  39.1 1.7 gather_fusion.8
  40.8 0.6 gather_fusion.9
  41.6 0.6 reshape.170.ids_ref
  42.3 0.8 sort.90
  43.3 1.7 gather_fusion.6
  45.1 0.6 gather_fusion.7
  45.8 0.7 reshape.169.ids_ref
  46.6 0.8 sort.89
  47.6 1.7 gather_fusion.4
  49.4 0.6 gather_fusion.5
  50.1 0.7 reshape.168.ids_ref
  50.9 0.8 sort.88
  51.9 1.7 gather_fusion.2
  53.6 0.6 gather_fusion.3
  55.1 0.8 sort.87
  56.1 1.7 gather_fusion
  57.9 0.6 gather_fusion.1
  59.8 1.1 copy-done.3
  60.9 2.6 pad_maximum_fusion.refs_0_.refs_1_
  63.4 2.0 fusion.6.q_ref
  65.4 42.0 %shard_map.64 = (f32[6,768,256]{2,1,0:T(8,128)}, f32[6,2,6,1,256]{4,3,2,1,0:T(1,128)}) custom-call(s32[162]{0:T(256)} %reshape.171.ids_ref, s32[6]{0:T(128)} %copy-done.12, bf16[768,1536]{1,0:T(8,128)(2,1)} %fusion.6.q_ref, bf16[2,1536,768]{2,1,0:T(8,128)(2,1)} %pad_maximum_fusion.refs_0_.refs_1_, bf16[2,1536,768]{2,1,0:T(8,128)(2,1)} %pad_maximum_fusion.refs_0_.refs_1_), custom_call_target="tpu_custom_call" | custom-call | tf_op jit(solution)/shard_map/pallas_call | solution.py:162
  107.5 34.4 %shard_map.65 = (f32[6,768,256]{2,1,0:T(8,128)}, f32[6,2,6,1,256]{4,3,2,1,0:T(1,128)}) custom-call(s32[162]{0:T(256)} %reshape.170.ids_ref, s32[6]{0:T(128)} %copy-done.11, bf16[768,1536]{1,0:T(8,128)(2,1)} %fusion.6.q_ref, bf16[2,2048,768]{2,1,0:T(8,128)(2,1)} %all-gather.14.cloned.1.call-done.refs_0_.refs_1_, ...), custom_call_target="tpu_custom_call" | custom-call | tf_op jit(solution)/shard_map/pallas_call | solution.py:162
  141.9 63.8 %all-gather.12.cloned.1.call-done.refs_0_.refs_1_ = bf16[2,4096,768]{2,1,0:T(8,128)(2,1)} async-done(((bf16[2,512,768]{2,1,0:T(8,128)(2,1)}), bf16[2,4096,768]{2,1,0:T(8,128)(2,1)}) %all-gather.12.cloned.1.call-update) | async-done | bytes 12582928 | tf_op jit(solution)/shard_map/all_gather | solution.py:255
  205.6 66.6 %shard_map.66 = (f32[6,768,256]{2,1,0:T(8,128)}, f32[6,2,6,1,256]{4,3,2,1,0:T(1,128)}) custom-call(s32[162]{0:T(256)} %reshape.169.ids_ref, s32[6]{0:T(128)} %copy-done.10, bf16[768,1536]{1,0:T(8,128)(2,1)} %fusion.6.q_ref, bf16[2,4096,768]{2,1,0:T(8,128)(2,1)} %all-gather.12.cloned.1.call-done.refs_0_.refs_1_, ...), custom_call_target="tpu_custom_call" | custom-call | tf_op jit(solution)/shard_map/pallas_call | solution.py:162
  272.3 45.7 %shard_map.67 = (f32[6,768,256]{2,1,0:T(8,128)}, f32[6,2,6,1,256]{4,3,2,1,0:T(1,128)}) custom-call(s32[162]{0:T(256)} %reshape.168.ids_ref, s32[6]{0:T(128)} %copy-done.9, bf16[768,1536]{1,0:T(8,128)(2,1)} %fusion.6.q_ref, bf16[2,2048,768]{2,1,0:T(8,128)(2,1)} %all-gather.10.cloned.1.call-done.refs_0_.refs_1_, ...), custom_call_target="tpu_custom_call" | custom-call | tf_op jit(solution)/shard_map/pallas_call | solution.py:162
  318.0 17.8 %all-gather.8.cloned.1.call-done.refs_0_.refs_1_ = bf16[2,2048,768]{2,1,0:T(8,128)(2,1)} async-done(((bf16[2,256,768]{2,1,0:T(8,128)(2,1)}), bf16[2,2048,768]{2,1,0:T(8,128)(2,1)}) %all-gather.8.cloned.1.call-update) | async-done | bytes 6291472 | tf_op jit(solution)/shard_map/all_gather | solution.py:255
  335.7 32.9 %shard_map.68 = (f32[6,768,256]{2,1,0:T(8,128)}, f32[6,2,6,1,256]{4,3,2,1,0:T(1,128)}) custom-call(s32[162]{0:T(256)} %reshape.167.ids_ref, s32[6]{0:T(128)} %copy-done.8, bf16[768,1536]{1,0:T(8,128)(2,1)} %fusion.6.q_ref, bf16[2,2048,768]{2,1,0:T(8,128)(2,1)} %all-gather.8.cloned.1.call-done.refs_0_.refs_1_, ...), custom_call_target="tpu_custom_call" | custom-call | tf_op jit(solution)/shard_map/pallas_call | solution.py:162
  368.6 32.0 %all-gather.6.cloned.1.call-done.refs_0_.refs_1_ = bf16[2,2048,768]{2,1,0:T(8,128)(2,1)} async-done(((bf16[2,256,768]{2,1,0:T(8,128)(2,1)}), bf16[2,2048,768]{2,1,0:T(8,128)(2,1)}) %all-gather.6.cloned.1.call-update) | async-done | bytes 6291472 | tf_op jit(solution)/shard_map/all_gather | solution.py:255
  400.6 40.5 %shard_map.69 = bf16[1536,768]{1,0:T(8,128)(2,1)} custom-call(s32[162]{0:T(256)} %reshape.166.ids_ref, s32[6]{0:T(128)} %copy-done.7, bf16[768,1536]{1,0:T(8,128)(2,1)} %fusion.6.q_ref, bf16[2,2048,768]{2,1,0:T(8,128)(2,1)} %all-gather.6.cloned.1.call-done.refs_0_.refs_1_, bf16[2,2048,768]{2,1,0:T(8,128)(2,1)} %all-gather.6.cloned.1.call-done.refs_0_.refs_1_, ...), custom_call_target="tpu_custom_call" | custom-call | tf_op jit(solution)/shard_map/pallas_call | solution.py:162
  (121 shorter events, 7.6 us)
Async XLA Ops:
  6.5 6.8 %copy-start = (bf16[1536,768]{1,0:T(8,128)(2,1)S(1)}, bf16[1536,768]{1,0:T(8,128)(2,1)}, u32[]{:S(2)}) copy-start(bf16[1536,768]{1,0:T(8,128)(2,1)} %param.11) | copy-start | bytes 7077892
  6.5 12.7 %copy-start.5 = (f32[768]{0:T(1024)S(1)}, f32[768]{0:T(1024)}, u32[]{:S(2)}) copy-start(f32[768]{0:T(1024)} %param.14) | copy-start | bytes 9220
  6.5 100.9 %all-gather.14.cloned.1.call-start = ((), (), s32[]{:S(2)}) async-start(), calls=%async_computation.4 | async-start | bytes 7077888 | tf_op jit(solution)/shard_map/all_gather | solution.py:255
  11.0 8.9 %copy-start.2 = (bf16[1536,768]{1,0:T(8,128)(2,1)S(1)}, bf16[1536,768]{1,0:T(8,128)(2,1)}, u32[]{:S(2)}) copy-start(bf16[1536,768]{1,0:T(8,128)(2,1)} %param.12) | copy-start | bytes 7077892
  13.9 2.6 collective-permute-start
  16.5 2.6 collective-permute-start.1
  19.8 1.8 copy-start.4
  22.6 183.0 %all-gather.12.cloned.1.call-start = ((), (), s32[]{:S(2)}) async-start(), calls=%async_computation.3 | async-start | bytes 14155776 | tf_op jit(solution)/shard_map/all_gather | solution.py:255
  26.4 245.9 %all-gather.10.cloned.1.call-start = ((), (), s32[]{:S(2)}) async-start(), calls=%async_computation.2 | async-start | bytes 7077888 | tf_op jit(solution)/shard_map/all_gather | solution.py:255
  28.6 307.2 %all-gather.8.cloned.1.call-start = ((), (), s32[]{:S(2)}) async-start(), calls=%async_computation.1 | async-start | bytes 7077888 | tf_op jit(solution)/shard_map/all_gather | solution.py:255
  30.6 370.0 %all-gather.6.cloned.1.call-start = ((), (), s32[]{:S(2)}) async-start(), calls=%async_computation | async-start | bytes 7077888 | tf_op jit(solution)/shard_map/all_gather | solution.py:255
  32.5 8.3 %copy-start.12 = (s32[6]{0:T(128)}, s32[6]{0:T(128)S(1)}, u32[]{:S(2)}) copy-start(s32[6]{0:T(128)S(1)} %get-tuple-element.41.cnt_ref) | copy-start | bytes 76
  34.5 7.0 %copy-start.11 = (s32[6]{0:T(128)}, s32[6]{0:T(128)S(1)}, u32[]{:S(2)}) copy-start(s32[6]{0:T(128)S(1)} %get-tuple-element.44.cnt_ref) | copy-start | bytes 76
  34.5 11.3 %copy-start.10 = (s32[6]{0:T(128)}, s32[6]{0:T(128)S(1)}, u32[]{:S(2)}) copy-start(s32[6]{0:T(128)S(1)} %get-tuple-element.64.cnt_ref) | copy-start | bytes 76
  34.5 15.6 %copy-start.9 = (s32[6]{0:T(128)}, s32[6]{0:T(128)S(1)}, u32[]{:S(2)}) copy-start(s32[6]{0:T(128)S(1)} %get-tuple-element.62.cnt_ref) | copy-start | bytes 76
  34.5 19.8 %copy-start.8 = (s32[6]{0:T(128)}, s32[6]{0:T(128)S(1)}, u32[]{:S(2)}) copy-start(s32[6]{0:T(128)S(1)} %get-tuple-element.66.cnt_ref) | copy-start | bytes 76
  34.5 24.0 %copy-start.7 = (s32[6]{0:T(128)}, s32[6]{0:T(128)S(1)}, u32[]{:S(2)}) copy-start(s32[6]{0:T(128)S(1)} %get-tuple-element.68.cnt_ref) | copy-start | bytes 76
  51.9 7.3 %copy-start.6 = (f32[768]{0:T(1024)S(1)}, f32[768]{0:T(1024)}, u32[]{:S(2)}) copy-start(f32[768]{0:T(1024)} %param.14) | copy-start | bytes 9220
  59.2 1.7 copy-start.3
  60.9 2.6 copy-start.1
  60.9 2.6 copy-start.13
Sparse Core Ops, SparseCore 0:
  22.7 66.4 all-gather.13
  90.8 114.8 all-gather.11
  207.3 63.4 all-gather.9
  272.3 63.3 all-gather.7
  337.2 63.3 all-gather.5

commit v4 on v3

--- a/solution.py
+++ b/solution.py
@@ -237,11 +237,11 @@
     local_tiles = rows // TILE_TOKENS
     tile_count = tok_count * local_tiles
     sizes = phase_sizes(local_tiles)
-    query_total, key_total = head_sums(
-        jnp.stack([square_sums(query_states), square_sums(key_states)]), head_count
-    )
-    query_normed = normalize_rows(query_states, query_total, query_gain)
+    key_total = head_sums(square_sums(key_states), head_count)
     sent_keys = normalize_rows(key_states, key_total, key_gain)
+    query_in, _ = lax.optimization_barrier((query_states, sent_keys))
+    query_total = head_sums(square_sums(query_in), head_count)
+    query_normed = normalize_rows(query_in, query_total, query_gain)
     query_t = query_normed.T
     shard = lax.axis_index("tok")
     own = jnp.stack([sent_keys, value_states])

time: 453 us -> 453 us (level); the launches traced: 448 us -> 454 us
  Pallas kernels: 262 us -> 328 us
  waiting for transfers between devices: 117 us -> 57.8 us
    pallas_call x6, Pallas kernels: 262 us -> 328 us  [window_attention(): pl.pallas_call(functools.partial(attention_kernel, first=first, last=last...]
    all_gather x5, waiting for transfers between devices: 114 us -> 52.2 us  [on_device(): extended = lax.all_gather(paired, 'tok', axis=1, tiled=True)]
    unnamed x29 -> x34, local copies, waits for them, and re-layouts: 6.03 us -> 1.48 us
  transfers between devices with their start and end apart: 7 -> 9, of which waited for: 5 -> 5; matrix products, arithmetic and copies ran while one was open for 9% -> 9% of each run, Pallas kernels for 50% -> 61%
where the time goes in v4:
time: 453 us; the launch traced here: 454 us
  Pallas kernels  328 us (72%)
  waiting for transfers between devices  57.8 us (13%)
  local copies, waits for them, and re-layouts  28 us (6%)
  other arithmetic  23.2 us (5%)
  between operations  13.6 us (3%)
    pallas_call x6, Pallas kernels, window_attention(): pl.pallas_call(functools.partial(attention_kernel, first=first, last=last...  328 us
    all_gather x5, waiting for transfers between devices, on_device(): extended = lax.all_gather(paired, 'tok', axis=1, tiled=True)  52.2 us
    gather x18, local copies, waits for them, and re-layouts, phase_windows(): ids = jnp.take_along_axis(block, order, axis=1)  10.9 us
  transfers between devices with their start and end apart: 9, of which 5 were waited for; matrix products, arithmetic and copies ran while one was open for 9% of the time, Pallas kernels for 61%

profile of v4, /device:TPU:11, one launch (start us, length us, event | category | flops | bytes accessed | tf_op | source)
XLA Modules:
  0.0 454.4 jit_solution(17506506522942851953)
XLA Ops:
  6.5 2.3 fusion
  9.2 2.2 collective-permute-done
  11.5 1.2 collective-permute-start.1
  12.7 1.3 collective-permute-done.1
  14.0 2.3 fusion.2
  16.3 1.4 copy-done.4
  17.7 1.1 slice_bitcast_fusion.2
  18.7 1.0 pad_maximum_fusion.5
  19.9 1.3 slice_bitcast_fusion
  21.2 1.3 pad_maximum_fusion.1
  22.6 1.0 pad_maximum_fusion.4
  23.7 1.0 pad_maximum_fusion.3
  24.9 1.0 pad_maximum_fusion.2
  26.1 0.8 sort.92
  27.4 1.7 gather_fusion.10
  29.2 0.6 gather_fusion.11
  30.0 0.7 reshape.147.ids_ref
  30.8 0.8 sort.91
  31.8 1.7 gather_fusion.8
  33.5 0.6 gather_fusion.9
  34.3 0.6 reshape.146.ids_ref
  35.0 0.8 sort.90
  36.0 1.7 gather_fusion.6
  37.8 0.6 gather_fusion.7
  38.5 0.7 reshape.145.ids_ref
  39.3 0.8 sort.89
  40.3 1.7 gather_fusion.4
  42.8 0.7 reshape.144.ids_ref
  43.6 0.8 sort.88
  44.6 1.7 gather_fusion.2
  46.4 0.6 gather_fusion.3
  47.8 0.8 sort.87
  48.8 1.7 gather_fusion
  50.6 0.6 gather_fusion.1
  52.0 4.3 copy.12
  56.2 2.3 fusion.3
  59.5 2.0 collective-permute-done.2
  61.5 1.2 collective-permute-start.3
  62.8 2.6 pad_maximum_fusion.refs_0_.refs_1_
  65.4 2.0 fusion.6.q_ref
  67.3 55.4 %shard_map.64 = (f32[6,768,256]{2,1,0:T(8,128)}, f32[6,2,6,1,256]{4,3,2,1,0:T(1,128)}) custom-call(s32[162]{0:T(256)} %reshape.147.ids_ref, s32[6]{0:T(128)} %copy-done.15, bf16[768,1536]{1,0:T(8,128)(2,1)} %fusion.6.q_ref, bf16[2,1536,768]{2,1,0:T(8,128)(2,1)} %pad_maximum_fusion.refs_0_.refs_1_, bf16[2,1536,768]{2,1,0:T(8,128)(2,1)} %pad_maximum_fusion.refs_0_.refs_1_), custom_call_target="tpu_custom_call" | custom-call | tf_op jit(solution)/shard_map/pallas_call | solution.py:162
  122.7 43.2 %shard_map.65 = (f32[6,768,256]{2,1,0:T(8,128)}, f32[6,2,6,1,256]{4,3,2,1,0:T(1,128)}) custom-call(s32[162]{0:T(256)} %reshape.146.ids_ref, s32[6]{0:T(128)} %copy-done.14, bf16[768,1536]{1,0:T(8,128)(2,1)} %fusion.6.q_ref, bf16[2,2048,768]{2,1,0:T(8,128)(2,1)} %all-gather.14.cloned.1.call-done.refs_0_.refs_1_, ...), custom_call_target="tpu_custom_call" | custom-call | tf_op jit(solution)/shard_map/pallas_call | solution.py:162
  165.9 36.9 %all-gather.12.cloned.1.call-done.refs_0_.refs_1_ = bf16[2,4096,768]{2,1,0:T(8,128)(2,1)} async-done(((bf16[2,512,768]{2,1,0:T(8,128)(2,1)}), bf16[2,4096,768]{2,1,0:T(8,128)(2,1)}) %all-gather.12.cloned.1.call-update) | async-done | bytes 12582928 | tf_op jit(solution)/shard_map/all_gather | solution.py:255
  202.8 90.3 %shard_map.66 = (f32[6,768,256]{2,1,0:T(8,128)}, f32[6,2,6,1,256]{4,3,2,1,0:T(1,128)}) custom-call(s32[162]{0:T(256)} %reshape.145.ids_ref, s32[6]{0:T(128)} %copy-done.13, bf16[768,1536]{1,0:T(8,128)(2,1)} %fusion.6.q_ref, bf16[2,4096,768]{2,1,0:T(8,128)(2,1)} %all-gather.12.cloned.1.call-done.refs_0_.refs_1_, ...), custom_call_target="tpu_custom_call" | custom-call | tf_op jit(solution)/shard_map/pallas_call | solution.py:162
  293.2 51.2 %shard_map.67 = (f32[6,768,256]{2,1,0:T(8,128)}, f32[6,2,6,1,256]{4,3,2,1,0:T(1,128)}) custom-call(s32[162]{0:T(256)} %reshape.144.ids_ref, s32[6]{0:T(128)} %copy-done.12, bf16[768,1536]{1,0:T(8,128)(2,1)} %fusion.6.q_ref, bf16[2,2048,768]{2,1,0:T(8,128)(2,1)} %all-gather.10.cloned.1.call-done.refs_0_.refs_1_, ...), custom_call_target="tpu_custom_call" | custom-call | tf_op jit(solution)/shard_map/pallas_call | solution.py:162
  344.4 38.1 %shard_map.68 = (f32[6,768,256]{2,1,0:T(8,128)}, f32[6,2,6,1,256]{4,3,2,1,0:T(1,128)}) custom-call(s32[162]{0:T(256)} %reshape.143.ids_ref, s32[6]{0:T(128)} %copy-done.11, bf16[768,1536]{1,0:T(8,128)(2,1)} %fusion.6.q_ref, bf16[2,2048,768]{2,1,0:T(8,128)(2,1)} %all-gather.8.cloned.1.call-done.refs_0_.refs_1_, ...), custom_call_target="tpu_custom_call" | custom-call | tf_op jit(solution)/shard_map/pallas_call | solution.py:162
  382.5 15.3 %all-gather.6.cloned.1.call-done.refs_0_.refs_1_ = bf16[2,2048,768]{2,1,0:T(8,128)(2,1)} async-done(((bf16[2,256,768]{2,1,0:T(8,128)(2,1)}), bf16[2,2048,768]{2,1,0:T(8,128)(2,1)}) %all-gather.6.cloned.1.call-update) | async-done | bytes 6291472 | tf_op jit(solution)/shard_map/all_gather | solution.py:255
  397.8 50.1 %shard_map.69 = bf16[1536,768]{1,0:T(8,128)(2,1)} custom-call(s32[162]{0:T(256)} %reshape.142.ids_ref, s32[6]{0:T(128)} %copy-done.10, bf16[768,1536]{1,0:T(8,128)(2,1)} %fusion.6.q_ref, bf16[2,2048,768]{2,1,0:T(8,128)(2,1)} %all-gather.6.cloned.1.call-done.refs_0_.refs_1_, bf16[2,2048,768]{2,1,0:T(8,128)(2,1)} %all-gather.6.cloned.1.call-done.refs_0_.refs_1_, ...), custom_call_target="tpu_custom_call" | custom-call | tf_op jit(solution)/shard_map/pallas_call | solution.py:162
  (129 shorter events, 6.8 us)
Async XLA Ops:
  6.5 11.1 %copy-start.2 = (bf16[1536,768]{1,0:T(8,128)(2,1)S(1)}, bf16[1536,768]{1,0:T(8,128)(2,1)}, u32[]{:S(2)}) copy-start(bf16[1536,768]{1,0:T(8,128)(2,1)} %param.12) | copy-start | bytes 7077892
  6.5 116.2 %all-gather.14.cloned.1.call-start = ((), (), s32[]{:S(2)}) async-start(), calls=%async_computation.4 | async-start | bytes 7077888 | tf_op jit(solution)/shard_map/all_gather | solution.py:255
  8.9 2.6 collective-permute-start
  11.5 2.5 collective-permute-start.1
  16.2 1.4 copy-start.4
  19.7 183.1 %all-gather.12.cloned.1.call-start = ((), (), s32[]{:S(2)}) async-start(), calls=%async_computation.3 | async-start | bytes 14155776 | tf_op jit(solution)/shard_map/all_gather | solution.py:255
  19.9 2.7 copy-start.6
  19.9 2.7 copy-start.7
  19.9 3.8 copy-start.5
  22.5 3.4 copy-start.8
  22.5 270.6 %all-gather.10.cloned.1.call-start = ((), (), s32[]{:S(2)}) async-start(), calls=%async_computation.2 | async-start | bytes 7077888 | tf_op jit(solution)/shard_map/all_gather | solution.py:255
  23.6 320.8 %all-gather.8.cloned.1.call-start = ((), (), s32[]{:S(2)}) async-start(), calls=%async_computation.1 | async-start | bytes 7077888 | tf_op jit(solution)/shard_map/all_gather | solution.py:255
  24.6 373.1 %all-gather.6.cloned.1.call-start = ((), (), s32[]{:S(2)}) async-start(), calls=%async_computation | async-start | bytes 7077888 | tf_op jit(solution)/shard_map/all_gather | solution.py:255
  26.0 7.4 %copy-start.15 = (s32[6]{0:T(128)}, s32[6]{0:T(128)S(1)}, u32[]{:S(2)}) copy-start(s32[6]{0:T(128)S(1)} %get-tuple-element.41.cnt_ref) | copy-start | bytes 76
  27.3 6.9 %copy-start.14 = (s32[6]{0:T(128)}, s32[6]{0:T(128)S(1)}, u32[]{:S(2)}) copy-start(s32[6]{0:T(128)S(1)} %get-tuple-element.44.cnt_ref) | copy-start | bytes 76
  27.3 11.1 %copy-start.13 = (s32[6]{0:T(128)}, s32[6]{0:T(128)S(1)}, u32[]{:S(2)}) copy-start(s32[6]{0:T(128)S(1)} %get-tuple-element.64.cnt_ref) | copy-start | bytes 76
  27.4 15.4 %copy-start.12 = (s32[6]{0:T(128)}, s32[6]{0:T(128)S(1)}, u32[]{:S(2)}) copy-start(s32[6]{0:T(128)S(1)} %get-tuple-element.62.cnt_ref) | copy-start | bytes 76
  27.4 19.7 %copy-start.11 = (s32[6]{0:T(128)}, s32[6]{0:T(128)S(1)}, u32[]{:S(2)}) copy-start(s32[6]{0:T(128)S(1)} %get-tuple-element.66.cnt_ref) | copy-start | bytes 76
  27.4 23.9 %copy-start.10 = (s32[6]{0:T(128)}, s32[6]{0:T(128)S(1)}, u32[]{:S(2)}) copy-start(s32[6]{0:T(128)S(1)} %get-tuple-element.68.cnt_ref) | copy-start | bytes 76
  50.5 8.4 %copy-start = (bf16[1536,768]{1,0:T(8,128)(2,1)S(1)}, bf16[1536,768]{1,0:T(8,128)(2,1)}, u32[]{:S(2)}) copy-start(bf16[1536,768]{1,0:T(8,128)(2,1)} %param.11) | copy-start | bytes 7077892
  50.5 8.4 %copy-start.9 = (f32[768]{0:T(1024)S(1)}, f32[768]{0:T(1024)}, u32[]{:S(2)}) copy-start(f32[768]{0:T(1024)} %param.14) | copy-start | bytes 9220
  56.2 6.5 %copy-start.3 = (bf16[1536,768]{1,0:T(8,128)(2,1)S(1)}, bf16[1536,768]{1,0:T(8,128)(2,1)}, u32[]{:S(2)}) copy-start(bf16[1536,768]{1,0:T(8,128)(2,1)} %param.12) | copy-start | bytes 7077892
  58.6 3.0 collective-permute-start.2
  61.5 3.8 collective-permute-start.3
  62.8 2.6 copy-start.1
  62.8 2.6 copy-start.16
Sparse Core Ops, SparseCore 0:
  19.9 66.4 all-gather.13
  87.9 114.8 all-gather.11
  204.4 63.5 all-gather.9
  269.4 63.3 all-gather.7
  334.3 63.3 all-gather.5

commit v5 on v4

--- a/solution.py
+++ b/solution.py
@@ -12,6 +12,7 @@
 MODEL_DIM = 3072
 TILE_TOKENS = 256
 WINDOW_SLOTS = 27
+LOG2_E = 1.4426950408889634
 FRAME_SLOTS = 9
 FRAME_ROWS = 4
 FRAME_COLS = 4
@@ -88,13 +89,13 @@
                     lax.dot_general(
                         k, q_t, (((1,), (0,)), ((), ())), preferred_element_type=jnp.float32
                     )
-                    * score_scale
+                    * (score_scale * LOG2_E)
                 )
                 m_prev = m_sc[h]
                 m_cur = jnp.max(scores, axis=0, keepdims=True)
                 m_new = jnp.maximum(m_prev, m_cur)
-                alpha = jnp.exp(m_prev - m_new)
-                weights = jnp.exp(scores - m_new)
+                alpha = jnp.exp2(m_prev - m_new)
+                weights = jnp.exp2(scores - m_new)
                 l_sc[h] = alpha * l_sc[h] + jnp.sum(weights, axis=0, keepdims=True)
                 m_sc[h] = m_new
                 mixed = lax.dot_general(

time: 453 us -> 454 us (level)
  Pallas kernels: 328 us -> 322 us
  waiting for transfers between devices: 57.8 us -> 63.3 us
    pallas_call x6, Pallas kernels: 328 us -> 322 us  [window_attention(): pl.pallas_call(functools.partial(attention_kernel, first=first, last=last...]
    all_gather x5, waiting for transfers between devices: 52.2 us -> 57.7 us  [on_device(): extended = lax.all_gather(paired, 'tok', axis=1, tiled=True)]
  transfers between devices with their start and end apart: 9 -> 9, of which waited for: 5 -> 5; matrix products, arithmetic and copies ran while one was open for 9% -> 9% of each run, Pallas kernels for 61% -> 60%
where the time goes in v5:
time: 454 us; the launch traced here: 453 us
  Pallas kernels  322 us (71%)
  waiting for transfers between devices  63.3 us (14%)
  local copies, waits for them, and re-layouts  28 us (6%)
  other arithmetic  23.2 us (5%)
  between operations  13.6 us (3%)
    pallas_call x6, Pallas kernels, window_attention(): pl.pallas_call(functools.partial(attention_kernel, first=first, last=last...  322 us
    all_gather x5, waiting for transfers between devices, on_device(): extended = lax.all_gather(paired, 'tok', axis=1, tiled=True)  57.7 us
    gather x18, local copies, waits for them, and re-layouts, phase_windows(): ids = jnp.take_along_axis(block, order, axis=1)  10.9 us
  transfers between devices with their start and end apart: 9, of which 5 were waited for; matrix products, arithmetic and copies ran while one was open for 9% of the time, Pallas kernels for 60%

profile of v5, /device:TPU:11, one launch (start us, length us, event | category | flops | bytes accessed | tf_op | source)
XLA Modules:
  0.0 453.4 jit_solution(1995205687288541834)
XLA Ops:
  6.5 2.3 fusion
  9.2 2.2 collective-permute-done
  11.5 1.2 collective-permute-start.1
  12.7 1.3 collective-permute-done.1
  14.0 2.3 fusion.2
  16.3 1.4 copy-done.4
  17.7 1.1 slice_bitcast_fusion.2
  18.7 1.0 pad_maximum_fusion.5
  19.9 1.3 slice_bitcast_fusion
  21.2 1.3 pad_maximum_fusion.1
  22.6 1.0 pad_maximum_fusion.4
  23.7 1.0 pad_maximum_fusion.3
  24.9 1.0 pad_maximum_fusion.2
  26.1 0.8 sort.92
  27.4 1.7 gather_fusion.10
  29.2 0.6 gather_fusion.11
  30.0 0.7 reshape.147.ids_ref
  30.8 0.8 sort.91
  31.8 1.7 gather_fusion.8
  34.3 0.6 reshape.146.ids_ref
  35.0 0.8 sort.90
  36.0 1.7 gather_fusion.6
  37.8 0.6 gather_fusion.7
  38.5 0.7 reshape.145.ids_ref
  39.3 0.8 sort.89
  40.3 1.7 gather_fusion.4
  42.1 0.6 gather_fusion.5
  42.8 0.7 reshape.144.ids_ref
  43.6 0.8 sort.88
  44.6 1.7 gather_fusion.2
  46.4 0.6 gather_fusion.3
  47.8 0.8 sort.87
  48.8 1.7 gather_fusion
  50.6 0.6 gather_fusion.1
  52.0 4.3 copy.12
  56.2 2.3 fusion.3
  59.5 2.0 collective-permute-done.2
  61.5 1.2 collective-permute-start.3
  62.8 2.6 pad_maximum_fusion.refs_0_.refs_1_
  65.4 2.0 fusion.6.q_ref
  67.3 51.9 %shard_map.64 = (f32[6,768,256]{2,1,0:T(8,128)}, f32[6,2,6,1,256]{4,3,2,1,0:T(1,128)}) custom-call(s32[162]{0:T(256)} %reshape.147.ids_ref, s32[6]{0:T(128)} %copy-done.15, bf16[768,1536]{1,0:T(8,128)(2,1)} %fusion.6.q_ref, bf16[2,1536,768]{2,1,0:T(8,128)(2,1)} %pad_maximum_fusion.refs_0_.refs_1_, bf16[2,1536,768]{2,1,0:T(8,128)(2,1)} %pad_maximum_fusion.refs_0_.refs_1_), custom_call_target="tpu_custom_call" | custom-call | tf_op jit(solution)/shard_map/pallas_call | solution.py:163
  119.2 42.7 %shard_map.65 = (f32[6,768,256]{2,1,0:T(8,128)}, f32[6,2,6,1,256]{4,3,2,1,0:T(1,128)}) custom-call(s32[162]{0:T(256)} %reshape.146.ids_ref, s32[6]{0:T(128)} %copy-done.14, bf16[768,1536]{1,0:T(8,128)(2,1)} %fusion.6.q_ref, bf16[2,2048,768]{2,1,0:T(8,128)(2,1)} %all-gather.14.cloned.1.call-done.refs_0_.refs_1_, ...), custom_call_target="tpu_custom_call" | custom-call | tf_op jit(solution)/shard_map/pallas_call | solution.py:163
  162.0 40.8 %all-gather.12.cloned.1.call-done.refs_0_.refs_1_ = bf16[2,4096,768]{2,1,0:T(8,128)(2,1)} async-done(((bf16[2,512,768]{2,1,0:T(8,128)(2,1)}), bf16[2,4096,768]{2,1,0:T(8,128)(2,1)}) %all-gather.12.cloned.1.call-update) | async-done | bytes 12582928 | tf_op jit(solution)/shard_map/all_gather | solution.py:256
  202.8 88.3 %shard_map.66 = (f32[6,768,256]{2,1,0:T(8,128)}, f32[6,2,6,1,256]{4,3,2,1,0:T(1,128)}) custom-call(s32[162]{0:T(256)} %reshape.145.ids_ref, s32[6]{0:T(128)} %copy-done.13, bf16[768,1536]{1,0:T(8,128)(2,1)} %fusion.6.q_ref, bf16[2,4096,768]{2,1,0:T(8,128)(2,1)} %all-gather.12.cloned.1.call-done.refs_0_.refs_1_, ...), custom_call_target="tpu_custom_call" | custom-call | tf_op jit(solution)/shard_map/pallas_call | solution.py:163
  291.1 48.5 %shard_map.67 = (f32[6,768,256]{2,1,0:T(8,128)}, f32[6,2,6,1,256]{4,3,2,1,0:T(1,128)}) custom-call(s32[162]{0:T(256)} %reshape.144.ids_ref, s32[6]{0:T(128)} %copy-done.12, bf16[768,1536]{1,0:T(8,128)(2,1)} %fusion.6.q_ref, bf16[2,2048,768]{2,1,0:T(8,128)(2,1)} %all-gather.10.cloned.1.call-done.refs_0_.refs_1_, ...), custom_call_target="tpu_custom_call" | custom-call | tf_op jit(solution)/shard_map/pallas_call | solution.py:163
  339.7 41.2 %shard_map.68 = (f32[6,768,256]{2,1,0:T(8,128)}, f32[6,2,6,1,256]{4,3,2,1,0:T(1,128)}) custom-call(s32[162]{0:T(256)} %reshape.143.ids_ref, s32[6]{0:T(128)} %copy-done.11, bf16[768,1536]{1,0:T(8,128)(2,1)} %fusion.6.q_ref, bf16[2,2048,768]{2,1,0:T(8,128)(2,1)} %all-gather.8.cloned.1.call-done.refs_0_.refs_1_, ...), custom_call_target="tpu_custom_call" | custom-call | tf_op jit(solution)/shard_map/pallas_call | solution.py:163
  380.9 16.9 %all-gather.6.cloned.1.call-done.refs_0_.refs_1_ = bf16[2,2048,768]{2,1,0:T(8,128)(2,1)} async-done(((bf16[2,256,768]{2,1,0:T(8,128)(2,1)}), bf16[2,2048,768]{2,1,0:T(8,128)(2,1)}) %all-gather.6.cloned.1.call-update) | async-done | bytes 6291472 | tf_op jit(solution)/shard_map/all_gather | solution.py:256
  397.8 49.2 %shard_map.69 = bf16[1536,768]{1,0:T(8,128)(2,1)} custom-call(s32[162]{0:T(256)} %reshape.142.ids_ref, s32[6]{0:T(128)} %copy-done.10, bf16[768,1536]{1,0:T(8,128)(2,1)} %fusion.6.q_ref, bf16[2,2048,768]{2,1,0:T(8,128)(2,1)} %all-gather.6.cloned.1.call-done.refs_0_.refs_1_, bf16[2,2048,768]{2,1,0:T(8,128)(2,1)} %all-gather.6.cloned.1.call-done.refs_0_.refs_1_, ...), custom_call_target="tpu_custom_call" | custom-call | tf_op jit(solution)/shard_map/pallas_call | solution.py:163
  (129 shorter events, 6.8 us)
Async XLA Ops:
  6.5 11.1 %copy-start.2 = (bf16[1536,768]{1,0:T(8,128)(2,1)S(1)}, bf16[1536,768]{1,0:T(8,128)(2,1)}, u32[]{:S(2)}) copy-start(bf16[1536,768]{1,0:T(8,128)(2,1)} %param.12) | copy-start | bytes 7077892
  6.5 112.7 %all-gather.14.cloned.1.call-start = ((), (), s32[]{:S(2)}) async-start(), calls=%async_computation.4 | async-start | bytes 7077888 | tf_op jit(solution)/shard_map/all_gather | solution.py:256
  8.9 2.6 collective-permute-start
  11.5 2.5 collective-permute-start.1
  16.2 1.4 copy-start.4
  19.7 183.1 %all-gather.12.cloned.1.call-start = ((), (), s32[]{:S(2)}) async-start(), calls=%async_computation.3 | async-start | bytes 14155776 | tf_op jit(solution)/shard_map/all_gather | solution.py:256
  19.9 2.7 copy-start.6
  19.9 2.7 copy-start.7
  19.9 3.8 copy-start.5
  22.5 3.4 copy-start.8
  22.5 268.6 %all-gather.10.cloned.1.call-start = ((), (), s32[]{:S(2)}) async-start(), calls=%async_computation.2 | async-start | bytes 7077888 | tf_op jit(solution)/shard_map/all_gather | solution.py:256
  23.6 316.1 %all-gather.8.cloned.1.call-start = ((), (), s32[]{:S(2)}) async-start(), calls=%async_computation.1 | async-start | bytes 7077888 | tf_op jit(solution)/shard_map/all_gather | solution.py:256
  24.6 373.1 %all-gather.6.cloned.1.call-start = ((), (), s32[]{:S(2)}) async-start(), calls=%async_computation | async-start | bytes 7077888 | tf_op jit(solution)/shard_map/all_gather | solution.py:256
  26.0 7.4 %copy-start.15 = (s32[6]{0:T(128)}, s32[6]{0:T(128)S(1)}, u32[]{:S(2)}) copy-start(s32[6]{0:T(128)S(1)} %get-tuple-element.41.cnt_ref) | copy-start | bytes 76
  27.3 6.9 %copy-start.14 = (s32[6]{0:T(128)}, s32[6]{0:T(128)S(1)}, u32[]{:S(2)}) copy-start(s32[6]{0:T(128)S(1)} %get-tuple-element.44.cnt_ref) | copy-start | bytes 76
  27.3 11.1 %copy-start.13 = (s32[6]{0:T(128)}, s32[6]{0:T(128)S(1)}, u32[]{:S(2)}) copy-start(s32[6]{0:T(128)S(1)} %get-tuple-element.64.cnt_ref) | copy-start | bytes 76
  27.4 15.4 %copy-start.12 = (s32[6]{0:T(128)}, s32[6]{0:T(128)S(1)}, u32[]{:S(2)}) copy-start(s32[6]{0:T(128)S(1)} %get-tuple-element.62.cnt_ref) | copy-start | bytes 76
  27.4 19.7 %copy-start.11 = (s32[6]{0:T(128)}, s32[6]{0:T(128)S(1)}, u32[]{:S(2)}) copy-start(s32[6]{0:T(128)S(1)} %get-tuple-element.66.cnt_ref) | copy-start | bytes 76
  27.4 23.9 %copy-start.10 = (s32[6]{0:T(128)}, s32[6]{0:T(128)S(1)}, u32[]{:S(2)}) copy-start(s32[6]{0:T(128)S(1)} %get-tuple-element.68.cnt_ref) | copy-start | bytes 76
  50.5 8.4 %copy-start = (bf16[1536,768]{1,0:T(8,128)(2,1)S(1)}, bf16[1536,768]{1,0:T(8,128)(2,1)}, u32[]{:S(2)}) copy-start(bf16[1536,768]{1,0:T(8,128)(2,1)} %param.11) | copy-start | bytes 7077892
  50.5 8.4 %copy-start.9 = (f32[768]{0:T(1024)S(1)}, f32[768]{0:T(1024)}, u32[]{:S(2)}) copy-start(f32[768]{0:T(1024)} %param.14) | copy-start | bytes 9220
  56.2 6.5 %copy-start.3 = (bf16[1536,768]{1,0:T(8,128)(2,1)S(1)}, bf16[1536,768]{1,0:T(8,128)(2,1)}, u32[]{:S(2)}) copy-start(bf16[1536,768]{1,0:T(8,128)(2,1)} %param.12) | copy-start | bytes 7077892
  58.6 3.0 collective-permute-start.2
  61.5 3.8 collective-permute-start.3
  62.8 2.6 copy-start.1
  62.8 2.6 copy-start.16
Sparse Core Ops, SparseCore 0:
  19.9 66.4 all-gather.13
  87.9 114.8 all-gather.11
  204.4 63.4 all-gather.9
  269.4 63.4 all-gather.7
  334.3 63.3 all-gather.5

commit v6 on v5

--- a/solution.py
+++ b/solution.py
@@ -217,8 +217,8 @@
 
 
 def phase_sizes(local_tiles):
-    if local_tiles >= 3:
-        return [1, 2] + [1] * (local_tiles - 3)
+    if local_tiles % 2 == 0 and local_tiles >= 4:
+        return [2] * (local_tiles // 2 - 1) + [1, 1]
     return [local_tiles]
 
 

time: 454 us -> 435 us (0.958)
  Pallas kernels: 322 us -> 311 us
    pallas_call x6 -> x5, Pallas kernels: 322 us -> 311 us  [window_attention(): pl.pallas_call(functools.partial(attention_kernel, first=first, last=last...]
    all_gather x5 -> x4, waiting for transfers between devices: 57.7 us -> 54.5 us  [on_device(): extended = lax.all_gather(paired, 'tok', axis=1, tiled=True)]
    gather x18 -> x15, local copies, waits for them, and re-layouts: 10.9 us -> 9.27 us  [phase_windows(): ids = jnp.take_along_axis(block, order, axis=1)]
  transfers between devices with their start and end apart: 9 -> 8, of which waited for: 5 -> 5; matrix products, arithmetic and copies ran while one was open for 9% -> 10% of each run, Pallas kernels for 60% -> 61%
where the time goes in v6:
time: 435 us
  Pallas kernels  311 us (71%)
  waiting for transfers between devices  58.9 us (14%)
  local copies, waits for them, and re-layouts  27.2 us (6%)
  other arithmetic  21.1 us (5%)
  between operations  13.5 us (3%)
    pallas_call x5, Pallas kernels, window_attention(): pl.pallas_call(functools.partial(attention_kernel, first=first, last=last...  311 us
    all_gather x4, waiting for transfers between devices, on_device(): extended = lax.all_gather(paired, 'tok', axis=1, tiled=True)  54.5 us
    gather x15, local copies, waits for them, and re-layouts, phase_windows(): ids = jnp.take_along_axis(block, order, axis=1)  9.27 us
  transfers between devices with their start and end apart: 8, of which 5 were waited for; matrix products, arithmetic and copies ran while one was open for 10% of the time, Pallas kernels for 61%

profile of v6, /device:TPU:11, one launch (start us, length us, event | category | flops | bytes accessed | tf_op | source)
XLA Modules:
  0.0 434.8 jit_solution(3660105760956428511)
XLA Ops:
  6.5 2.3 fusion
  8.9 0.3 collective-permute-start
  9.2 2.2 collective-permute-done
  11.5 1.2 collective-permute-start.1
  12.7 1.5 slice_bitcast_fusion.2
  14.2 0.6 fusion.2
  14.8 1.4 copy-done.2
  16.2 1.0 slice_bitcast_fusion
  17.2 1.3 pad_maximum_fusion.2
  18.6 2.5 pad_maximum_fusion.1
  21.2 1.2 slice_bitcast_fusion.6
  22.3 1.2 slice_bitcast_fusion.4
  23.5 1.0 pad_maximum_fusion.4
  24.6 1.0 pad_maximum_fusion.3
  25.8 0.8 sort.77
  27.0 1.8 gather_fusion.8
  29.0 0.6 gather_fusion.9
  29.8 0.7 reshape.128.ids_ref
  30.5 0.8 sort.76
  31.5 1.7 gather_fusion.6
  33.3 0.6 gather_fusion.7
  34.0 0.7 reshape.127.ids_ref
  34.8 0.8 sort.75
  35.8 1.7 gather_fusion.4
  37.6 0.6 gather_fusion.5
  38.3 0.7 reshape.126.ids_ref
  39.1 0.8 sort.74
  40.1 1.7 gather_fusion.2
  41.9 0.6 gather_fusion.3
  42.6 0.6 reshape.125.ids_ref
  43.3 0.8 sort.73
  44.3 1.7 gather_fusion
  46.1 0.6 gather_fusion.1
  46.8 0.6 reshape.124.ids_ref
  47.4 4.3 copy.12
  51.7 2.3 fusion.3
  54.4 0.6 fusion.23
  55.0 2.0 collective-permute-done.2
  57.0 1.0 collective-permute-start.3
  58.0 2.6 pad_maximum_fusion.refs_0_.refs_1_
  60.6 2.0 fusion.6.q_ref
  62.6 48.7 %shard_map.64 = (f32[6,768,256]{2,1,0:T(8,128)}, f32[6,2,6,1,256]{4,3,2,1,0:T(1,128)}) custom-call(s32[162]{0:T(256)} %reshape.128.ids_ref, s32[6]{0:T(128)} %copy-done.10, bf16[768,1536]{1,0:T(8,128)(2,1)} %fusion.6.q_ref, bf16[2,1536,768]{2,1,0:T(8,128)(2,1)} %pad_maximum_fusion.refs_0_.refs_1_, bf16[2,1536,768]{2,1,0:T(8,128)(2,1)} %pad_maximum_fusion.refs_0_.refs_1_), custom_call_target="tpu_custom_call" | custom-call | tf_op jit(solution)/shard_map/pallas_call | solution.py:163
  111.3 25.0 %all-gather.11.cloned.1.call-done.refs_0_.refs_1_ = bf16[2,4096,768]{2,1,0:T(8,128)(2,1)} async-done(((bf16[2,512,768]{2,1,0:T(8,128)(2,1)}), bf16[2,4096,768]{2,1,0:T(8,128)(2,1)}) %all-gather.11.cloned.1.call-update) | async-done | bytes 12582928 | tf_op jit(solution)/shard_map/all_gather | solution.py:256
  136.3 87.1 %shard_map.65 = (f32[6,768,256]{2,1,0:T(8,128)}, f32[6,2,6,1,256]{4,3,2,1,0:T(1,128)}) custom-call(s32[162]{0:T(256)} %reshape.127.ids_ref, s32[6]{0:T(128)} %copy-done.9, bf16[768,1536]{1,0:T(8,128)(2,1)} %fusion.6.q_ref, bf16[2,4096,768]{2,1,0:T(8,128)(2,1)} %all-gather.11.cloned.1.call-done.refs_0_.refs_1_, ...), custom_call_target="tpu_custom_call" | custom-call | tf_op jit(solution)/shard_map/pallas_call | solution.py:163
  223.4 29.4 %all-gather.9.cloned.1.call-done.refs_0_.refs_1_ = bf16[2,4096,768]{2,1,0:T(8,128)(2,1)} async-done(((bf16[2,512,768]{2,1,0:T(8,128)(2,1)}), bf16[2,4096,768]{2,1,0:T(8,128)(2,1)}) %all-gather.9.cloned.1.call-update) | async-done | bytes 12582928 | tf_op jit(solution)/shard_map/all_gather | solution.py:256
  252.9 83.4 %shard_map.66 = (f32[6,768,256]{2,1,0:T(8,128)}, f32[6,2,6,1,256]{4,3,2,1,0:T(1,128)}) custom-call(s32[162]{0:T(256)} %reshape.126.ids_ref, s32[6]{0:T(128)} %copy-done.8, bf16[768,1536]{1,0:T(8,128)(2,1)} %fusion.6.q_ref, bf16[2,4096,768]{2,1,0:T(8,128)(2,1)} %all-gather.9.cloned.1.call-done.refs_0_.refs_1_, ...), custom_call_target="tpu_custom_call" | custom-call | tf_op jit(solution)/shard_map/pallas_call | solution.py:163
  336.3 46.5 %shard_map.67 = (f32[6,768,256]{2,1,0:T(8,128)}, f32[6,2,6,1,256]{4,3,2,1,0:T(1,128)}) custom-call(s32[162]{0:T(256)} %reshape.125.ids_ref, s32[6]{0:T(128)} %copy-done.7, bf16[768,1536]{1,0:T(8,128)(2,1)} %fusion.6.q_ref, bf16[2,2048,768]{2,1,0:T(8,128)(2,1)} %all-gather.7.cloned.1.call-done.refs_0_.refs_1_, ...), custom_call_target="tpu_custom_call" | custom-call | tf_op jit(solution)/shard_map/pallas_call | solution.py:163
  382.9 45.3 %shard_map.68 = bf16[1536,768]{1,0:T(8,128)(2,1)} custom-call(s32[162]{0:T(256)} %reshape.124.ids_ref, s32[6]{0:T(128)} %copy-done.6, bf16[768,1536]{1,0:T(8,128)(2,1)} %fusion.6.q_ref, bf16[2,2048,768]{2,1,0:T(8,128)(2,1)} %all-gather.5.cloned.1.call-done.refs_0_.refs_1_, bf16[2,2048,768]{2,1,0:T(8,128)(2,1)} %all-gather.5.cloned.1.call-done.refs_0_.refs_1_, ...), custom_call_target="tpu_custom_call" | custom-call | tf_op jit(solution)/shard_map/pallas_call | solution.py:163
  (100 shorter events, 3.3 us)
Async XLA Ops:
  6.5 7.7 %copy-start = (bf16[1536,768]{1,0:T(8,128)(2,1)S(1)}, bf16[1536,768]{1,0:T(8,128)(2,1)}, u32[]{:S(2)}) copy-start(bf16[1536,768]{1,0:T(8,128)(2,1)} %param.11) | copy-start | bytes 7077892
  6.5 7.7 %copy-start.5 = (f32[768]{0:T(1024)S(1)}, f32[768]{0:T(1024)}, u32[]{:S(2)}) copy-start(f32[768]{0:T(1024)} %param.14) | copy-start | bytes 9220
  6.5 129.8 %all-gather.11.cloned.1.call-start = ((), (), s32[]{:S(2)}) async-start(), calls=%async_computation.3 | async-start | bytes 14155776 | tf_op jit(solution)/shard_map/all_gather | solution.py:256
  8.9 2.6 collective-permute-start
  11.5 2.7 collective-permute-start.1
  14.8 1.4 copy-start.2
  18.5 234.3 %all-gather.9.cloned.1.call-start = ((), (), s32[]{:S(2)}) async-start(), calls=%async_computation.2 | async-start | bytes 14155776 | tf_op jit(solution)/shard_map/all_gather | solution.py:256
  21.1 4.5 %copy-start.4 = (s32[6,27]{1,0:T(8,128)S(1)}, s32[6,27]{1,0:T(8,128)}, u32[]{:S(2)}) copy-start(s32[6,27]{1,0:T(8,128)} %param.15) | copy-start | bytes 1948
  21.1 315.2 %all-gather.7.cloned.1.call-start = ((), (), s32[]{:S(2)}) async-start(), calls=%async_computation.1 | async-start | bytes 7077888 | tf_op jit(solution)/shard_map/all_gather | solution.py:256
  24.5 358.4 %all-gather.5.cloned.1.call-start = ((), (), s32[]{:S(2)}) async-start(), calls=%async_computation | async-start | bytes 7077888 | tf_op jit(solution)/shard_map/all_gather | solution.py:256
  25.7 7.5 %copy-start.10 = (s32[6]{0:T(128)}, s32[6]{0:T(128)S(1)}, u32[]{:S(2)}) copy-start(s32[6]{0:T(128)S(1)} %get-tuple-element.35.cnt_ref) | copy-start | bytes 76
  27.0 7.0 %copy-start.9 = (s32[6]{0:T(128)}, s32[6]{0:T(128)S(1)}, u32[]{:S(2)}) copy-start(s32[6]{0:T(128)S(1)} %get-tuple-element.38.cnt_ref) | copy-start | bytes 76
  27.0 11.3 %copy-start.8 = (s32[6]{0:T(128)}, s32[6]{0:T(128)S(1)}, u32[]{:S(2)}) copy-start(s32[6]{0:T(128)S(1)} %get-tuple-element.56.cnt_ref) | copy-start | bytes 76
  27.0 15.5 %copy-start.7 = (s32[6]{0:T(128)}, s32[6]{0:T(128)S(1)}, u32[]{:S(2)}) copy-start(s32[6]{0:T(128)S(1)} %get-tuple-element.54.cnt_ref) | copy-start | bytes 76
  27.0 19.7 %copy-start.6 = (s32[6]{0:T(128)}, s32[6]{0:T(128)S(1)}, u32[]{:S(2)}) copy-start(s32[6]{0:T(128)S(1)} %get-tuple-element.58.cnt_ref) | copy-start | bytes 76
  51.7 6.3 %copy-start.3 = (bf16[1536,768]{1,0:T(8,128)(2,1)S(1)}, bf16[1536,768]{1,0:T(8,128)(2,1)}, u32[]{:S(2)}) copy-start(bf16[1536,768]{1,0:T(8,128)(2,1)} %param.12) | copy-start | bytes 7077892
  54.1 3.0 collective-permute-start.2
  57.0 3.5 collective-permute-start.3
  58.0 2.6 copy-start.1
  58.0 2.6 copy-start.11
Sparse Core Ops, SparseCore 0:
  18.7 117.6 all-gather.10
  137.9 114.8 all-gather.8
  254.5 63.5 all-gather.6
  319.6 63.3 all-gather.4
